TPU v7x, 256 devices: a whole 4x4x8 slice. The times are simulated.
256 devices in a mesh: seq: 32 (over z_lo, y, core), head: 8 (over x, z_hi).
Axes of the slice: x: 4, y: 4, z: 8 (z_hi: 2, z_lo: 4; z = z_hi * 4 + z_lo), core: 2. Of those that a mesh axis runs over, the one named last changes fastest.
Arguments:
- queries: bfloat16 [16384, 1024], P('seq', 'head'), may hold values from -2.5 to 2.5
- keys: bfloat16 [16384, 1024], P('seq', 'head'), may hold values from -2.5 to 2.5
- values: bfloat16 [16384, 1024], P('seq', 'head'), may hold values from -6 to 6
- attn_out: bfloat16 [16384, 1024], P('seq', 'head'), may hold values from -6 to 6
- out_grad: bfloat16 [16384, 1024], P('seq', 'head'), may hold values from -6 to 6
- lse: float32 [8, 16384], P('head', 'seq'), may hold values from 3.5 to 5.5
- trace_id: int32 [16384], replicated, may hold values from 0 to 127, never falling along the last dimension, each value on 1 to 384 neighbouring positions
- key_tiles: int32 [128, 48], P('seq'), may hold values from 0 to 127, as said below
- tile_count: int32 [128], P('seq'), may hold values from 1 to 48, as said below
- w_query: bfloat16 [1024, 1024], P(None, 'head'), may hold values from -0.1875 to 0.1875
- w_key: bfloat16 [1024, 1024], P(None, 'head'), may hold values from -0.1875 to 0.1875
- w_value: bfloat16 [1024, 1024], P(None, 'head'), may hold values from -0.1875 to 0.1875
- w_out: bfloat16 [1024, 1024], P('head'), may hold values from -0.1875 to 0.1875
Outputs:
- d_input: bfloat16 [16384, 1024], P('seq', 'head')
Inputs may be any that keep to these rules, and one draw needn't show every extreme that they name: `key_tiles`: each row lists 48 different key tiles and never its own tile; entries from position tile_count onward are not used. `tile_count`: some query tile uses all 48 entries. `trace_id`: trace numbers never fall along the tokens; one trace spans 384 tokens, none more.
All inputs are finite; a program needn't handle non-finite values.
Results may differ from a plain program's by a relative error of at most 0.015.
Values may be sent and summed in bfloat16 or wider, within the bound.
No kernel may reach another device: no remote copies, remote signals or barrier semaphores. Data moves between devices by JAX's collectives and lax.ppermute only.
A program may use at most 64 MiB of HBM per device.

v0:
```python
import jax
import jax.numpy as jnp
from jax import lax
from jax.sharding import PartitionSpec as P

HD = 128
TILE = 128
SEL = 48


def from_behind(value, axis, by):
    count = lax.axis_size(axis)
    return lax.ppermute(value, axis, [(i, (i + by) % count) for i in range(count)])


def pair_grads(query_heads, key_heads, value_heads, grad_heads, norm_rows, delta_rows, admit):
    scale = query_heads.shape[-1] ** (-0.5)
    scores = (
        jnp.einsum("rhd,chd->hrc", query_heads, key_heads, preferred_element_type=jnp.float32)
        * scale
    )
    probs = jnp.where(admit[None], jnp.exp(scores - norm_rows[:, :, None]), 0.0)
    value_grad = jnp.einsum(
        "hrc,rhd->chd", probs.astype(jnp.bfloat16), grad_heads, preferred_element_type=jnp.float32
    )
    prob_grad = jnp.einsum(
        "rhd,chd->hrc", grad_heads, value_heads, preferred_element_type=jnp.float32
    )
    score_grad = (probs * (prob_grad - delta_rows[:, :, None]) * scale).astype(jnp.bfloat16)
    query_grad = jnp.einsum(
        "hrc,chd->rhd", score_grad, key_heads, preferred_element_type=jnp.float32
    )
    key_grad = jnp.einsum(
        "hrc,rhd->chd", score_grad, query_heads, preferred_element_type=jnp.float32
    )
    return (query_grad, key_grad, value_grad)


def settle(total):
    part = lax.optimization_barrier(total.astype(jnp.bfloat16))
    return part.astype(jnp.float32)


def per_device(
    queries,
    keys,
    values,
    attn_out,
    out_grad,
    lse,
    trace_id,
    key_tiles,
    tile_count,
    w_query,
    w_key,
    w_value,
    w_out,
):
    tokens_here, width = queries.shape
    heads_here = width // HD
    seq_count = lax.axis_size("seq")
    seq_index = lax.axis_index("seq")
    tiles_here = tokens_here // TILE
    d_attn = lax.dot_general(
        lax.all_gather(out_grad, "head", axis=1, tiled=True),
        w_out,
        (((1,), (1,)), ((), ())),
        preferred_element_type=jnp.float32,
    ).astype(jnp.bfloat16)
    product = d_attn.astype(jnp.float32) * attn_out.astype(jnp.float32)
    delta = jnp.sum(product.reshape(tokens_here, heads_here, HD), axis=2).T
    query_heads = queries.reshape(tokens_here, heads_here, HD)
    key_heads = keys.reshape(tokens_here, heads_here, HD)
    value_heads = values.reshape(tokens_here, heads_here, HD)
    grad_heads = d_attn.reshape(tokens_here, heads_here, HD)
    trace_here = lax.dynamic_slice_in_dim(trace_id, seq_index * tokens_here, tokens_here, 0)
    slots = jnp.arange(SEL)[None, :] < tile_count[:, None]
    tile_range = jnp.arange(seq_count * tiles_here)
    allowed = jnp.any(
        (key_tiles[:, :, None] == tile_range[None, None, :]) & slots[:, :, None], axis=1
    )

    def visit(key_block, value_block, first_tile):
        block_tiles = key_block.shape[0] // TILE
        listed = lax.dynamic_slice(allowed, (0, first_tile), (tiles_here, block_tiles))
        trace_keys = lax.dynamic_slice_in_dim(trace_id, first_tile * TILE, key_block.shape[0], 0)
        admit = jnp.repeat(jnp.repeat(listed, TILE, axis=0), TILE, axis=1) & (
            trace_here[:, None] != trace_keys[None, :]
        )
        return pair_grads(query_heads, key_block, value_block, grad_heads, lse, delta, admit)

    zero_rows = jnp.zeros((tokens_here, heads_here, HD), jnp.float32)

    def pass_sums(sums):
        return from_behind(sums, "seq", 1)

    def cycle_work(step, held, sums, query_sum):
        source = (seq_index - step) % seq_count
        query_add, key_add, value_add = visit(held[0], held[1], source * tiles_here)
        return (query_sum + query_add, sums + jnp.stack([settle(key_add), settle(value_add)]))

    def cycle_turn(step, carry):
        held, sums, query_sum = carry
        query_sum, sums = cycle_work(step, held, sums, query_sum)
        held = from_behind(held, "seq", 1)
        return (held, pass_sums(sums), query_sum)

    start_carry = (
        jnp.stack([key_heads, value_heads]),
        jnp.stack([zero_rows, zero_rows]),
        zero_rows,
    )
    held, sums, query_sum = lax.fori_loop(0, seq_count - 1, cycle_turn, start_carry)
    query_sum, sums = cycle_work(seq_count - 1, held, sums, query_sum)
    sums = pass_sums(sums)
    key_sum, value_sum = (sums[0], sums[1])
    d_query = query_sum.astype(jnp.bfloat16).reshape(tokens_here, width)
    d_key = key_sum.astype(jnp.bfloat16).reshape(tokens_here, width)
    d_value = value_sum.astype(jnp.bfloat16).reshape(tokens_here, width)
    contract = (((1,), (1,)), ((), ()))
    total = lax.dot_general(w_query, d_query, contract, preferred_element_type=jnp.float32)
    total = total + lax.dot_general(w_key, d_key, contract, preferred_element_type=jnp.float32)
    d_input = lax.psum_scatter(
        total + lax.dot_general(w_value, d_value, contract, preferred_element_type=jnp.float32),
        "head",
        scatter_dimension=0,
        tiled=True,
    )
    return d_input.T.astype(jnp.bfloat16)


def solution(mesh):
    in_specs = (
        P("seq", "head"),
        P("seq", "head"),
        P("seq", "head"),
        P("seq", "head"),
        P("seq", "head"),
        P("head", "seq"),
        P(),
        P("seq", None),
        P("seq"),
        P(None, "head"),
        P(None, "head"),
        P(None, "head"),
        P("head", None),
    )
    out_specs = P("seq", "head")
    return jax.shard_map(
        per_device, mesh=mesh, in_specs=in_specs, out_specs=out_specs, check_vma=False
    )
```

profile of v0, /device:TPU:32, one launch (start us, length us, event | category | flops | bytes accessed | tf_op | source)
XLA Modules:
  0.0 789.5 jit_solution(7173864981957476666)
XLA Ops:
  12.3 60.7 %all-gather.2.cloned.1.call-done = bf16[512,1024]{1,0:T(8,128)(2,1)} async-done(((bf16[512,128]{1,0:T(8,128)(2,1)}), bf16[512,1024]{1,0:T(8,128)(2,1)}) %all-gather.2.cloned.1.call-update) | async-done | bytes 1048592 | tf_op jit(solution)/shard_map/all_gather | solution.py:65
  75.0 548.2 %while.20 = (s32[]{:T(128)}, bf16[2,512,1,128]{3,1,2,0:T(8,128)(2,1)S(1)}, f32[2,512,1,128]{3,1,2,0:T(8,128)S(1)}, f32[512,1,128]{2,0,1:T(8,128)S(1)}, s32[]{:T(...) while((s32[]{:T(128)}, ...), condition=%wide.region_3.4_spmd.clone, body=%wide.region_2.3_spmd.clone.sunk | while | flops 338821152 | bytes 11944476 | solution.py:113
  97.3 13.1 %collective-permute-done = bf16[2,512,1,128]{3,1,2,0:T(8,128)(2,1)S(1)} collective-permute-done((bf16[2,512,1,128]{3,1,2,0:T(8,128)(2,1)S(1)}, bf16[2,512,1,128]{3,1,2,0:T(8,128)(2,1)S(1)}, u32[]{:S(2)}, u32[]{:S(2)}) %collective-permute-start) | collective-permute-done | bytes 262176 | tf_op jit(solution)/shard_map/while/body/eval_jaxpr/ppermute | solution.py:13
  115.0 13.1 %collective-permute-done = bf16[2,512,1,128]{3,1,2,0:T(8,128)(2,1)S(1)} collective-permute-done((bf16[2,512,1,128]{3,1,2,0:T(8,128)(2,1)S(1)}, bf16[2,512,1,128]{3,1,2,0:T(8,128)(2,1)S(1)}, u32[]{:S(2)}, u32[]{:S(2)}) %collective-permute-start) | collective-permute-done | bytes 262176 | tf_op jit(solution)/shard_map/while/body/eval_jaxpr/ppermute | solution.py:13
  132.7 13.1 %collective-permute-done = bf16[2,512,1,128]{3,1,2,0:T(8,128)(2,1)S(1)} collective-permute-done((bf16[2,512,1,128]{3,1,2,0:T(8,128)(2,1)S(1)}, bf16[2,512,1,128]{3,1,2,0:T(8,128)(2,1)S(1)}, u32[]{:S(2)}, u32[]{:S(2)}) %collective-permute-start) | collective-permute-done | bytes 262176 | tf_op jit(solution)/shard_map/while/body/eval_jaxpr/ppermute | solution.py:13
  150.3 13.1 %collective-permute-done = bf16[2,512,1,128]{3,1,2,0:T(8,128)(2,1)S(1)} collective-permute-done((bf16[2,512,1,128]{3,1,2,0:T(8,128)(2,1)S(1)}, bf16[2,512,1,128]{3,1,2,0:T(8,128)(2,1)S(1)}, u32[]{:S(2)}, u32[]{:S(2)}) %collective-permute-start) | collective-permute-done | bytes 262176 | tf_op jit(solution)/shard_map/while/body/eval_jaxpr/ppermute | solution.py:13
  168.0 13.1 %collective-permute-done = bf16[2,512,1,128]{3,1,2,0:T(8,128)(2,1)S(1)} collective-permute-done((bf16[2,512,1,128]{3,1,2,0:T(8,128)(2,1)S(1)}, bf16[2,512,1,128]{3,1,2,0:T(8,128)(2,1)S(1)}, u32[]{:S(2)}, u32[]{:S(2)}) %collective-permute-start) | collective-permute-done | bytes 262176 | tf_op jit(solution)/shard_map/while/body/eval_jaxpr/ppermute | solution.py:13
  185.7 13.1 %collective-permute-done = bf16[2,512,1,128]{3,1,2,0:T(8,128)(2,1)S(1)} collective-permute-done((bf16[2,512,1,128]{3,1,2,0:T(8,128)(2,1)S(1)}, bf16[2,512,1,128]{3,1,2,0:T(8,128)(2,1)S(1)}, u32[]{:S(2)}, u32[]{:S(2)}) %collective-permute-start) | collective-permute-done | bytes 262176 | tf_op jit(solution)/shard_map/while/body/eval_jaxpr/ppermute | solution.py:13
  203.4 13.1 %collective-permute-done = bf16[2,512,1,128]{3,1,2,0:T(8,128)(2,1)S(1)} collective-permute-done((bf16[2,512,1,128]{3,1,2,0:T(8,128)(2,1)S(1)}, bf16[2,512,1,128]{3,1,2,0:T(8,128)(2,1)S(1)}, u32[]{:S(2)}, u32[]{:S(2)}) %collective-permute-start) | collective-permute-done | bytes 262176 | tf_op jit(solution)/shard_map/while/body/eval_jaxpr/ppermute | solution.py:13
  221.1 13.1 %collective-permute-done = bf16[2,512,1,128]{3,1,2,0:T(8,128)(2,1)S(1)} collective-permute-done((bf16[2,512,1,128]{3,1,2,0:T(8,128)(2,1)S(1)}, bf16[2,512,1,128]{3,1,2,0:T(8,128)(2,1)S(1)}, u32[]{:S(2)}, u32[]{:S(2)}) %collective-permute-start) | collective-permute-done | bytes 262176 | tf_op jit(solution)/shard_map/while/body/eval_jaxpr/ppermute | solution.py:13
  238.8 13.1 %collective-permute-done = bf16[2,512,1,128]{3,1,2,0:T(8,128)(2,1)S(1)} collective-permute-done((bf16[2,512,1,128]{3,1,2,0:T(8,128)(2,1)S(1)}, bf16[2,512,1,128]{3,1,2,0:T(8,128)(2,1)S(1)}, u32[]{:S(2)}, u32[]{:S(2)}) %collective-permute-start) | collective-permute-done | bytes 262176 | tf_op jit(solution)/shard_map/while/body/eval_jaxpr/ppermute | solution.py:13
  256.5 13.1 %collective-permute-done = bf16[2,512,1,128]{3,1,2,0:T(8,128)(2,1)S(1)} collective-permute-done((bf16[2,512,1,128]{3,1,2,0:T(8,128)(2,1)S(1)}, bf16[2,512,1,128]{3,1,2,0:T(8,128)(2,1)S(1)}, u32[]{:S(2)}, u32[]{:S(2)}) %collective-permute-start) | collective-permute-done | bytes 262176 | tf_op jit(solution)/shard_map/while/body/eval_jaxpr/ppermute | solution.py:13
  274.1 13.1 %collective-permute-done = bf16[2,512,1,128]{3,1,2,0:T(8,128)(2,1)S(1)} collective-permute-done((bf16[2,512,1,128]{3,1,2,0:T(8,128)(2,1)S(1)}, bf16[2,512,1,128]{3,1,2,0:T(8,128)(2,1)S(1)}, u32[]{:S(2)}, u32[]{:S(2)}) %collective-permute-start) | collective-permute-done | bytes 262176 | tf_op jit(solution)/shard_map/while/body/eval_jaxpr/ppermute | solution.py:13
  291.8 13.1 %collective-permute-done = bf16[2,512,1,128]{3,1,2,0:T(8,128)(2,1)S(1)} collective-permute-done((bf16[2,512,1,128]{3,1,2,0:T(8,128)(2,1)S(1)}, bf16[2,512,1,128]{3,1,2,0:T(8,128)(2,1)S(1)}, u32[]{:S(2)}, u32[]{:S(2)}) %collective-permute-start) | collective-permute-done | bytes 262176 | tf_op jit(solution)/shard_map/while/body/eval_jaxpr/ppermute | solution.py:13
  309.5 13.1 %collective-permute-done = bf16[2,512,1,128]{3,1,2,0:T(8,128)(2,1)S(1)} collective-permute-done((bf16[2,512,1,128]{3,1,2,0:T(8,128)(2,1)S(1)}, bf16[2,512,1,128]{3,1,2,0:T(8,128)(2,1)S(1)}, u32[]{:S(2)}, u32[]{:S(2)}) %collective-permute-start) | collective-permute-done | bytes 262176 | tf_op jit(solution)/shard_map/while/body/eval_jaxpr/ppermute | solution.py:13
  327.2 13.1 %collective-permute-done = bf16[2,512,1,128]{3,1,2,0:T(8,128)(2,1)S(1)} collective-permute-done((bf16[2,512,1,128]{3,1,2,0:T(8,128)(2,1)S(1)}, bf16[2,512,1,128]{3,1,2,0:T(8,128)(2,1)S(1)}, u32[]{:S(2)}, u32[]{:S(2)}) %collective-permute-start) | collective-permute-done | bytes 262176 | tf_op jit(solution)/shard_map/while/body/eval_jaxpr/ppermute | solution.py:13
  344.9 13.1 %collective-permute-done = bf16[2,512,1,128]{3,1,2,0:T(8,128)(2,1)S(1)} collective-permute-done((bf16[2,512,1,128]{3,1,2,0:T(8,128)(2,1)S(1)}, bf16[2,512,1,128]{3,1,2,0:T(8,128)(2,1)S(1)}, u32[]{:S(2)}, u32[]{:S(2)}) %collective-permute-start) | collective-permute-done | bytes 262176 | tf_op jit(solution)/shard_map/while/body/eval_jaxpr/ppermute | solution.py:13
  362.6 13.1 %collective-permute-done = bf16[2,512,1,128]{3,1,2,0:T(8,128)(2,1)S(1)} collective-permute-done((bf16[2,512,1,128]{3,1,2,0:T(8,128)(2,1)S(1)}, bf16[2,512,1,128]{3,1,2,0:T(8,128)(2,1)S(1)}, u32[]{:S(2)}, u32[]{:S(2)}) %collective-permute-start) | collective-permute-done | bytes 262176 | tf_op jit(solution)/shard_map/while/body/eval_jaxpr/ppermute | solution.py:13
  380.2 13.1 %collective-permute-done = bf16[2,512,1,128]{3,1,2,0:T(8,128)(2,1)S(1)} collective-permute-done((bf16[2,512,1,128]{3,1,2,0:T(8,128)(2,1)S(1)}, bf16[2,512,1,128]{3,1,2,0:T(8,128)(2,1)S(1)}, u32[]{:S(2)}, u32[]{:S(2)}) %collective-permute-start) | collective-permute-done | bytes 262176 | tf_op jit(solution)/shard_map/while/body/eval_jaxpr/ppermute | solution.py:13
  397.9 13.1 %collective-permute-done = bf16[2,512,1,128]{3,1,2,0:T(8,128)(2,1)S(1)} collective-permute-done((bf16[2,512,1,128]{3,1,2,0:T(8,128)(2,1)S(1)}, bf16[2,512,1,128]{3,1,2,0:T(8,128)(2,1)S(1)}, u32[]{:S(2)}, u32[]{:S(2)}) %collective-permute-start) | collective-permute-done | bytes 262176 | tf_op jit(solution)/shard_map/while/body/eval_jaxpr/ppermute | solution.py:13
  415.6 13.1 %collective-permute-done = bf16[2,512,1,128]{3,1,2,0:T(8,128)(2,1)S(1)} collective-permute-done((bf16[2,512,1,128]{3,1,2,0:T(8,128)(2,1)S(1)}, bf16[2,512,1,128]{3,1,2,0:T(8,128)(2,1)S(1)}, u32[]{:S(2)}, u32[]{:S(2)}) %collective-permute-start) | collective-permute-done | bytes 262176 | tf_op jit(solution)/shard_map/while/body/eval_jaxpr/ppermute | solution.py:13
  433.3 13.1 %collective-permute-done = bf16[2,512,1,128]{3,1,2,0:T(8,128)(2,1)S(1)} collective-permute-done((bf16[2,512,1,128]{3,1,2,0:T(8,128)(2,1)S(1)}, bf16[2,512,1,128]{3,1,2,0:T(8,128)(2,1)S(1)}, u32[]{:S(2)}, u32[]{:S(2)}) %collective-permute-start) | collective-permute-done | bytes 262176 | tf_op jit(solution)/shard_map/while/body/eval_jaxpr/ppermute | solution.py:13
  451.0 13.1 %collective-permute-done = bf16[2,512,1,128]{3,1,2,0:T(8,128)(2,1)S(1)} collective-permute-done((bf16[2,512,1,128]{3,1,2,0:T(8,128)(2,1)S(1)}, bf16[2,512,1,128]{3,1,2,0:T(8,128)(2,1)S(1)}, u32[]{:S(2)}, u32[]{:S(2)}) %collective-permute-start) | collective-permute-done | bytes 262176 | tf_op jit(solution)/shard_map/while/body/eval_jaxpr/ppermute | solution.py:13
  468.7 13.1 %collective-permute-done = bf16[2,512,1,128]{3,1,2,0:T(8,128)(2,1)S(1)} collective-permute-done((bf16[2,512,1,128]{3,1,2,0:T(8,128)(2,1)S(1)}, bf16[2,512,1,128]{3,1,2,0:T(8,128)(2,1)S(1)}, u32[]{:S(2)}, u32[]{:S(2)}) %collective-permute-start) | collective-permute-done | bytes 262176 | tf_op jit(solution)/shard_map/while/body/eval_jaxpr/ppermute | solution.py:13
  486.3 13.1 %collective-permute-done = bf16[2,512,1,128]{3,1,2,0:T(8,128)(2,1)S(1)} collective-permute-done((bf16[2,512,1,128]{3,1,2,0:T(8,128)(2,1)S(1)}, bf16[2,512,1,128]{3,1,2,0:T(8,128)(2,1)S(1)}, u32[]{:S(2)}, u32[]{:S(2)}) %collective-permute-start) | collective-permute-done | bytes 262176 | tf_op jit(solution)/shard_map/while/body/eval_jaxpr/ppermute | solution.py:13
  504.0 13.1 %collective-permute-done = bf16[2,512,1,128]{3,1,2,0:T(8,128)(2,1)S(1)} collective-permute-done((bf16[2,512,1,128]{3,1,2,0:T(8,128)(2,1)S(1)}, bf16[2,512,1,128]{3,1,2,0:T(8,128)(2,1)S(1)}, u32[]{:S(2)}, u32[]{:S(2)}) %collective-permute-start) | collective-permute-done | bytes 262176 | tf_op jit(solution)/shard_map/while/body/eval_jaxpr/ppermute | solution.py:13
  521.7 13.1 %collective-permute-done = bf16[2,512,1,128]{3,1,2,0:T(8,128)(2,1)S(1)} collective-permute-done((bf16[2,512,1,128]{3,1,2,0:T(8,128)(2,1)S(1)}, bf16[2,512,1,128]{3,1,2,0:T(8,128)(2,1)S(1)}, u32[]{:S(2)}, u32[]{:S(2)}) %collective-permute-start) | collective-permute-done | bytes 262176 | tf_op jit(solution)/shard_map/while/body/eval_jaxpr/ppermute | solution.py:13
  539.4 13.1 %collective-permute-done = bf16[2,512,1,128]{3,1,2,0:T(8,128)(2,1)S(1)} collective-permute-done((bf16[2,512,1,128]{3,1,2,0:T(8,128)(2,1)S(1)}, bf16[2,512,1,128]{3,1,2,0:T(8,128)(2,1)S(1)}, u32[]{:S(2)}, u32[]{:S(2)}) %collective-permute-start) | collective-permute-done | bytes 262176 | tf_op jit(solution)/shard_map/while/body/eval_jaxpr/ppermute | solution.py:13
  557.1 13.1 %collective-permute-done = bf16[2,512,1,128]{3,1,2,0:T(8,128)(2,1)S(1)} collective-permute-done((bf16[2,512,1,128]{3,1,2,0:T(8,128)(2,1)S(1)}, bf16[2,512,1,128]{3,1,2,0:T(8,128)(2,1)S(1)}, u32[]{:S(2)}, u32[]{:S(2)}) %collective-permute-start) | collective-permute-done | bytes 262176 | tf_op jit(solution)/shard_map/while/body/eval_jaxpr/ppermute | solution.py:13
  574.8 13.1 %collective-permute-done = bf16[2,512,1,128]{3,1,2,0:T(8,128)(2,1)S(1)} collective-permute-done((bf16[2,512,1,128]{3,1,2,0:T(8,128)(2,1)S(1)}, bf16[2,512,1,128]{3,1,2,0:T(8,128)(2,1)S(1)}, u32[]{:S(2)}, u32[]{:S(2)}) %collective-permute-start) | collective-permute-done | bytes 262176 | tf_op jit(solution)/shard_map/while/body/eval_jaxpr/ppermute | solution.py:13
  610.1 13.1 %collective-permute-done = bf16[2,512,1,128]{3,1,2,0:T(8,128)(2,1)S(1)} collective-permute-done((bf16[2,512,1,128]{3,1,2,0:T(8,128)(2,1)S(1)}, bf16[2,512,1,128]{3,1,2,0:T(8,128)(2,1)S(1)}, u32[]{:S(2)}, u32[]{:S(2)}) %collective-permute-start) | collective-permute-done | bytes 262176 | tf_op jit(solution)/shard_map/while/body/eval_jaxpr/ppermute | solution.py:13
  635.0 146.1 %reduce-scatter.2.cloned.1.call-done = f32[128,512]{0,1:T(8,128)} async-done(((f32[1024,512]{0,1:T(8,128)}), f32[128,512]{0,1:T(8,128)}) %reduce-scatter.2.cloned.1.call-update) | async-done | bytes 262160 | tf_op jit(solution)/shard_map/reduce_scatter | solution.py:123
  (478 shorter events, 187.0 us)
Async XLA Ops:
  6.5 66.5 %all-gather.2.cloned.1.call-start = ((), (), s32[]{:S(2)}) async-start(), calls=%async_computation.1 | async-start | bytes 1179648 | tf_op jit(solution)/shard_map/all_gather | solution.py:65
  7.3 773.8 %reduce-scatter.2.cloned.1.call-start = ((), (), s32[]{:S(2)}) async-start(), calls=%async_computation.2 | async-start | bytes 2359296 | tf_op jit(solution)/shard_map/reduce_scatter | solution.py:123
  79.1 13.6 %collective-permute-start.1 = (f32[2,512,1,128]{3,1,2,0:T(8,128)S(1)}, f32[2,512,1,128]{3,1,2,0:T(8,128)S(1)}, u32[]{:S(2)}, u32[]{:S(2)}) collective-permute-start(f32[2,512,1,128]{3,1,2,0:T(8,128)S(1)} %convert_add_fusion.3), channel_id=1, source_target_pairs={{0,8},{8,16},{16,24},{24,32},{32,40},{40,48},{48,56},{56,64},{64,7... | collective-permute-start | bytes 1572872 | tf_op jit(solution)/shard_map/while/body/eval_jaxpr/ppermute | solution.py:13
  96.8 13.6 %collective-permute-start.1 = (f32[2,512,1,128]{3,1,2,0:T(8,128)S(1)}, f32[2,512,1,128]{3,1,2,0:T(8,128)S(1)}, u32[]{:S(2)}, u32[]{:S(2)}) collective-permute-start(f32[2,512,1,128]{3,1,2,0:T(8,128)S(1)} %convert_add_fusion.3), channel_id=1, source_target_pairs={{0,8},{8,16},{16,24},{24,32},{32,40},{40,48},{48,56},{56,64},{64,7... | collective-permute-start | bytes 1572872 | tf_op jit(solution)/shard_map/while/body/eval_jaxpr/ppermute | solution.py:13
  114.5 13.6 %collective-permute-start.1 = (f32[2,512,1,128]{3,1,2,0:T(8,128)S(1)}, f32[2,512,1,128]{3,1,2,0:T(8,128)S(1)}, u32[]{:S(2)}, u32[]{:S(2)}) collective-permute-start(f32[2,512,1,128]{3,1,2,0:T(8,128)S(1)} %convert_add_fusion.3), channel_id=1, source_target_pairs={{0,8},{8,16},{16,24},{24,32},{32,40},{40,48},{48,56},{56,64},{64,7... | collective-permute-start | bytes 1572872 | tf_op jit(solution)/shard_map/while/body/eval_jaxpr/ppermute | solution.py:13
  132.1 13.6 %collective-permute-start.1 = (f32[2,512,1,128]{3,1,2,0:T(8,128)S(1)}, f32[2,512,1,128]{3,1,2,0:T(8,128)S(1)}, u32[]{:S(2)}, u32[]{:S(2)}) collective-permute-start(f32[2,512,1,128]{3,1,2,0:T(8,128)S(1)} %convert_add_fusion.3), channel_id=1, source_target_pairs={{0,8},{8,16},{16,24},{24,32},{32,40},{40,48},{48,56},{56,64},{64,7... | collective-permute-start | bytes 1572872 | tf_op jit(solution)/shard_map/while/body/eval_jaxpr/ppermute | solution.py:13
  149.8 13.6 %collective-permute-start.1 = (f32[2,512,1,128]{3,1,2,0:T(8,128)S(1)}, f32[2,512,1,128]{3,1,2,0:T(8,128)S(1)}, u32[]{:S(2)}, u32[]{:S(2)}) collective-permute-start(f32[2,512,1,128]{3,1,2,0:T(8,128)S(1)} %convert_add_fusion.3), channel_id=1, source_target_pairs={{0,8},{8,16},{16,24},{24,32},{32,40},{40,48},{48,56},{56,64},{64,7... | collective-permute-start | bytes 1572872 | tf_op jit(solution)/shard_map/while/body/eval_jaxpr/ppermute | solution.py:13
  167.5 13.6 %collective-permute-start.1 = (f32[2,512,1,128]{3,1,2,0:T(8,128)S(1)}, f32[2,512,1,128]{3,1,2,0:T(8,128)S(1)}, u32[]{:S(2)}, u32[]{:S(2)}) collective-permute-start(f32[2,512,1,128]{3,1,2,0:T(8,128)S(1)} %convert_add_fusion.3), channel_id=1, source_target_pairs={{0,8},{8,16},{16,24},{24,32},{32,40},{40,48},{48,56},{56,64},{64,7... | collective-permute-start | bytes 1572872 | tf_op jit(solution)/shard_map/while/body/eval_jaxpr/ppermute | solution.py:13
  185.2 13.6 %collective-permute-start.1 = (f32[2,512,1,128]{3,1,2,0:T(8,128)S(1)}, f32[2,512,1,128]{3,1,2,0:T(8,128)S(1)}, u32[]{:S(2)}, u32[]{:S(2)}) collective-permute-start(f32[2,512,1,128]{3,1,2,0:T(8,128)S(1)} %convert_add_fusion.3), channel_id=1, source_target_pairs={{0,8},{8,16},{16,24},{24,32},{32,40},{40,48},{48,56},{56,64},{64,7... | collective-permute-start | bytes 1572872 | tf_op jit(solution)/shard_map/while/body/eval_jaxpr/ppermute | solution.py:13
  202.9 13.6 %collective-permute-start.1 = (f32[2,512,1,128]{3,1,2,0:T(8,128)S(1)}, f32[2,512,1,128]{3,1,2,0:T(8,128)S(1)}, u32[]{:S(2)}, u32[]{:S(2)}) collective-permute-start(f32[2,512,1,128]{3,1,2,0:T(8,128)S(1)} %convert_add_fusion.3), channel_id=1, source_target_pairs={{0,8},{8,16},{16,24},{24,32},{32,40},{40,48},{48,56},{56,64},{64,7... | collective-permute-start | bytes 1572872 | tf_op jit(solution)/shard_map/while/body/eval_jaxpr/ppermute | solution.py:13
  220.6 13.6 %collective-permute-start.1 = (f32[2,512,1,128]{3,1,2,0:T(8,128)S(1)}, f32[2,512,1,128]{3,1,2,0:T(8,128)S(1)}, u32[]{:S(2)}, u32[]{:S(2)}) collective-permute-start(f32[2,512,1,128]{3,1,2,0:T(8,128)S(1)} %convert_add_fusion.3), channel_id=1, source_target_pairs={{0,8},{8,16},{16,24},{24,32},{32,40},{40,48},{48,56},{56,64},{64,7... | collective-permute-start | bytes 1572872 | tf_op jit(solution)/shard_map/while/body/eval_jaxpr/ppermute | solution.py:13
  238.2 13.6 %collective-permute-start.1 = (f32[2,512,1,128]{3,1,2,0:T(8,128)S(1)}, f32[2,512,1,128]{3,1,2,0:T(8,128)S(1)}, u32[]{:S(2)}, u32[]{:S(2)}) collective-permute-start(f32[2,512,1,128]{3,1,2,0:T(8,128)S(1)} %convert_add_fusion.3), channel_id=1, source_target_pairs={{0,8},{8,16},{16,24},{24,32},{32,40},{40,48},{48,56},{56,64},{64,7... | collective-permute-start | bytes 1572872 | tf_op jit(solution)/shard_map/while/body/eval_jaxpr/ppermute | solution.py:13
  255.9 13.6 %collective-permute-start.1 = (f32[2,512,1,128]{3,1,2,0:T(8,128)S(1)}, f32[2,512,1,128]{3,1,2,0:T(8,128)S(1)}, u32[]{:S(2)}, u32[]{:S(2)}) collective-permute-start(f32[2,512,1,128]{3,1,2,0:T(8,128)S(1)} %convert_add_fusion.3), channel_id=1, source_target_pairs={{0,8},{8,16},{16,24},{24,32},{32,40},{40,48},{48,56},{56,64},{64,7... | collective-permute-start | bytes 1572872 | tf_op jit(solution)/shard_map/while/body/eval_jaxpr/ppermute | solution.py:13
  273.6 13.6 %collective-permute-start.1 = (f32[2,512,1,128]{3,1,2,0:T(8,128)S(1)}, f32[2,512,1,128]{3,1,2,0:T(8,128)S(1)}, u32[]{:S(2)}, u32[]{:S(2)}) collective-permute-start(f32[2,512,1,128]{3,1,2,0:T(8,128)S(1)} %convert_add_fusion.3), channel_id=1, source_target_pairs={{0,8},{8,16},{16,24},{24,32},{32,40},{40,48},{48,56},{56,64},{64,7... | collective-permute-start | bytes 1572872 | tf_op jit(solution)/shard_map/while/body/eval_jaxpr/ppermute | solution.py:13
  291.3 13.6 %collective-permute-start.1 = (f32[2,512,1,128]{3,1,2,0:T(8,128)S(1)}, f32[2,512,1,128]{3,1,2,0:T(8,128)S(1)}, u32[]{:S(2)}, u32[]{:S(2)}) collective-permute-start(f32[2,512,1,128]{3,1,2,0:T(8,128)S(1)} %convert_add_fusion.3), channel_id=1, source_target_pairs={{0,8},{8,16},{16,24},{24,32},{32,40},{40,48},{48,56},{56,64},{64,7... | collective-permute-start | bytes 1572872 | tf_op jit(solution)/shard_map/while/body/eval_jaxpr/ppermute | solution.py:13
  309.0 13.6 %collective-permute-start.1 = (f32[2,512,1,128]{3,1,2,0:T(8,128)S(1)}, f32[2,512,1,128]{3,1,2,0:T(8,128)S(1)}, u32[]{:S(2)}, u32[]{:S(2)}) collective-permute-start(f32[2,512,1,128]{3,1,2,0:T(8,128)S(1)} %convert_add_fusion.3), channel_id=1, source_target_pairs={{0,8},{8,16},{16,24},{24,32},{32,40},{40,48},{48,56},{56,64},{64,7... | collective-permute-start | bytes 1572872 | tf_op jit(solution)/shard_map/while/body/eval_jaxpr/ppermute | solution.py:13
  326.7 13.6 %collective-permute-start.1 = (f32[2,512,1,128]{3,1,2,0:T(8,128)S(1)}, f32[2,512,1,128]{3,1,2,0:T(8,128)S(1)}, u32[]{:S(2)}, u32[]{:S(2)}) collective-permute-start(f32[2,512,1,128]{3,1,2,0:T(8,128)S(1)} %convert_add_fusion.3), channel_id=1, source_target_pairs={{0,8},{8,16},{16,24},{24,32},{32,40},{40,48},{48,56},{56,64},{64,7... | collective-permute-start | bytes 1572872 | tf_op jit(solution)/shard_map/while/body/eval_jaxpr/ppermute | solution.py:13
  344.4 13.6 %collective-permute-start.1 = (f32[2,512,1,128]{3,1,2,0:T(8,128)S(1)}, f32[2,512,1,128]{3,1,2,0:T(8,128)S(1)}, u32[]{:S(2)}, u32[]{:S(2)}) collective-permute-start(f32[2,512,1,128]{3,1,2,0:T(8,128)S(1)} %convert_add_fusion.3), channel_id=1, source_target_pairs={{0,8},{8,16},{16,24},{24,32},{32,40},{40,48},{48,56},{56,64},{64,7... | collective-permute-start | bytes 1572872 | tf_op jit(solution)/shard_map/while/body/eval_jaxpr/ppermute | solution.py:13
  362.0 13.6 %collective-permute-start.1 = (f32[2,512,1,128]{3,1,2,0:T(8,128)S(1)}, f32[2,512,1,128]{3,1,2,0:T(8,128)S(1)}, u32[]{:S(2)}, u32[]{:S(2)}) collective-permute-start(f32[2,512,1,128]{3,1,2,0:T(8,128)S(1)} %convert_add_fusion.3), channel_id=1, source_target_pairs={{0,8},{8,16},{16,24},{24,32},{32,40},{40,48},{48,56},{56,64},{64,7... | collective-permute-start | bytes 1572872 | tf_op jit(solution)/shard_map/while/body/eval_jaxpr/ppermute | solution.py:13
  379.7 13.6 %collective-permute-start.1 = (f32[2,512,1,128]{3,1,2,0:T(8,128)S(1)}, f32[2,512,1,128]{3,1,2,0:T(8,128)S(1)}, u32[]{:S(2)}, u32[]{:S(2)}) collective-permute-start(f32[2,512,1,128]{3,1,2,0:T(8,128)S(1)} %convert_add_fusion.3), channel_id=1, source_target_pairs={{0,8},{8,16},{16,24},{24,32},{32,40},{40,48},{48,56},{56,64},{64,7... | collective-permute-start | bytes 1572872 | tf_op jit(solution)/shard_map/while/body/eval_jaxpr/ppermute | solution.py:13
  397.4 13.6 %collective-permute-start.1 = (f32[2,512,1,128]{3,1,2,0:T(8,128)S(1)}, f32[2,512,1,128]{3,1,2,0:T(8,128)S(1)}, u32[]{:S(2)}, u32[]{:S(2)}) collective-permute-start(f32[2,512,1,128]{3,1,2,0:T(8,128)S(1)} %convert_add_fusion.3), channel_id=1, source_target_pairs={{0,8},{8,16},{16,24},{24,32},{32,40},{40,48},{48,56},{56,64},{64,7... | collective-permute-start | bytes 1572872 | tf_op jit(solution)/shard_map/while/body/eval_jaxpr/ppermute | solution.py:13
  415.1 13.6 %collective-permute-start.1 = (f32[2,512,1,128]{3,1,2,0:T(8,128)S(1)}, f32[2,512,1,128]{3,1,2,0:T(8,128)S(1)}, u32[]{:S(2)}, u32[]{:S(2)}) collective-permute-start(f32[2,512,1,128]{3,1,2,0:T(8,128)S(1)} %convert_add_fusion.3), channel_id=1, source_target_pairs={{0,8},{8,16},{16,24},{24,32},{32,40},{40,48},{48,56},{56,64},{64,7... | collective-permute-start | bytes 1572872 | tf_op jit(solution)/shard_map/while/body/eval_jaxpr/ppermute | solution.py:13
  432.8 13.6 %collective-permute-start.1 = (f32[2,512,1,128]{3,1,2,0:T(8,128)S(1)}, f32[2,512,1,128]{3,1,2,0:T(8,128)S(1)}, u32[]{:S(2)}, u32[]{:S(2)}) collective-permute-start(f32[2,512,1,128]{3,1,2,0:T(8,128)S(1)} %convert_add_fusion.3), channel_id=1, source_target_pairs={{0,8},{8,16},{16,24},{24,32},{32,40},{40,48},{48,56},{56,64},{64,7... | collective-permute-start | bytes 1572872 | tf_op jit(solution)/shard_map/while/body/eval_jaxpr/ppermute | solution.py:13
  450.5 13.6 %collective-permute-start.1 = (f32[2,512,1,128]{3,1,2,0:T(8,128)S(1)}, f32[2,512,1,128]{3,1,2,0:T(8,128)S(1)}, u32[]{:S(2)}, u32[]{:S(2)}) collective-permute-start(f32[2,512,1,128]{3,1,2,0:T(8,128)S(1)} %convert_add_fusion.3), channel_id=1, source_target_pairs={{0,8},{8,16},{16,24},{24,32},{32,40},{40,48},{48,56},{56,64},{64,7... | collective-permute-start | bytes 1572872 | tf_op jit(solution)/shard_map/while/body/eval_jaxpr/ppermute | solution.py:13
  468.1 13.6 %collective-permute-start.1 = (f32[2,512,1,128]{3,1,2,0:T(8,128)S(1)}, f32[2,512,1,128]{3,1,2,0:T(8,128)S(1)}, u32[]{:S(2)}, u32[]{:S(2)}) collective-permute-start(f32[2,512,1,128]{3,1,2,0:T(8,128)S(1)} %convert_add_fusion.3), channel_id=1, source_target_pairs={{0,8},{8,16},{16,24},{24,32},{32,40},{40,48},{48,56},{56,64},{64,7... | collective-permute-start | bytes 1572872 | tf_op jit(solution)/shard_map/while/body/eval_jaxpr/ppermute | solution.py:13
  485.8 13.6 %collective-permute-start.1 = (f32[2,512,1,128]{3,1,2,0:T(8,128)S(1)}, f32[2,512,1,128]{3,1,2,0:T(8,128)S(1)}, u32[]{:S(2)}, u32[]{:S(2)}) collective-permute-start(f32[2,512,1,128]{3,1,2,0:T(8,128)S(1)} %convert_add_fusion.3), channel_id=1, source_target_pairs={{0,8},{8,16},{16,24},{24,32},{32,40},{40,48},{48,56},{56,64},{64,7... | collective-permute-start | bytes 1572872 | tf_op jit(solution)/shard_map/while/body/eval_jaxpr/ppermute | solution.py:13
  503.5 13.6 %collective-permute-start.1 = (f32[2,512,1,128]{3,1,2,0:T(8,128)S(1)}, f32[2,512,1,128]{3,1,2,0:T(8,128)S(1)}, u32[]{:S(2)}, u32[]{:S(2)}) collective-permute-start(f32[2,512,1,128]{3,1,2,0:T(8,128)S(1)} %convert_add_fusion.3), channel_id=1, source_target_pairs={{0,8},{8,16},{16,24},{24,32},{32,40},{40,48},{48,56},{56,64},{64,7... | collective-permute-start | bytes 1572872 | tf_op jit(solution)/shard_map/while/body/eval_jaxpr/ppermute | solution.py:13
  521.2 13.6 %collective-permute-start.1 = (f32[2,512,1,128]{3,1,2,0:T(8,128)S(1)}, f32[2,512,1,128]{3,1,2,0:T(8,128)S(1)}, u32[]{:S(2)}, u32[]{:S(2)}) collective-permute-start(f32[2,512,1,128]{3,1,2,0:T(8,128)S(1)} %convert_add_fusion.3), channel_id=1, source_target_pairs={{0,8},{8,16},{16,24},{24,32},{32,40},{40,48},{48,56},{56,64},{64,7... | collective-permute-start | bytes 1572872 | tf_op jit(solution)/shard_map/while/body/eval_jaxpr/ppermute | solution.py:13
  538.9 13.6 %collective-permute-start.1 = (f32[2,512,1,128]{3,1,2,0:T(8,128)S(1)}, f32[2,512,1,128]{3,1,2,0:T(8,128)S(1)}, u32[]{:S(2)}, u32[]{:S(2)}) collective-permute-start(f32[2,512,1,128]{3,1,2,0:T(8,128)S(1)} %convert_add_fusion.3), channel_id=1, source_target_pairs={{0,8},{8,16},{16,24},{24,32},{32,40},{40,48},{48,56},{56,64},{64,7... | collective-permute-start | bytes 1572872 | tf_op jit(solution)/shard_map/while/body/eval_jaxpr/ppermute | solution.py:13
  556.6 13.6 %collective-permute-start.1 = (f32[2,512,1,128]{3,1,2,0:T(8,128)S(1)}, f32[2,512,1,128]{3,1,2,0:T(8,128)S(1)}, u32[]{:S(2)}, u32[]{:S(2)}) collective-permute-start(f32[2,512,1,128]{3,1,2,0:T(8,128)S(1)} %convert_add_fusion.3), channel_id=1, source_target_pairs={{0,8},{8,16},{16,24},{24,32},{32,40},{40,48},{48,56},{56,64},{64,7... | collective-permute-start | bytes 1572872 | tf_op jit(solution)/shard_map/while/body/eval_jaxpr/ppermute | solution.py:13
  574.2 13.6 %collective-permute-start.1 = (f32[2,512,1,128]{3,1,2,0:T(8,128)S(1)}, f32[2,512,1,128]{3,1,2,0:T(8,128)S(1)}, u32[]{:S(2)}, u32[]{:S(2)}) collective-permute-start(f32[2,512,1,128]{3,1,2,0:T(8,128)S(1)} %convert_add_fusion.3), channel_id=1, source_target_pairs={{0,8},{8,16},{16,24},{24,32},{32,40},{40,48},{48,56},{56,64},{64,7... | collective-permute-start | bytes 1572872 | tf_op jit(solution)/shard_map/while/body/eval_jaxpr/ppermute | solution.py:13
  591.9 13.6 %collective-permute-start.1 = (f32[2,512,1,128]{3,1,2,0:T(8,128)S(1)}, f32[2,512,1,128]{3,1,2,0:T(8,128)S(1)}, u32[]{:S(2)}, u32[]{:S(2)}) collective-permute-start(f32[2,512,1,128]{3,1,2,0:T(8,128)S(1)} %convert_add_fusion.3), channel_id=1, source_target_pairs={{0,8},{8,16},{16,24},{24,32},{32,40},{40,48},{48,56},{56,64},{64,7... | collective-permute-start | bytes 1572872 | tf_op jit(solution)/shard_map/while/body/eval_jaxpr/ppermute | solution.py:13
  (39 other events, 1218.4 us)
Sparse Core Ops, SparseCore 0:
  9.8 63.1 all-gather.1
  635.1 145.9 reduce-scatter.1
where the time goes:
time: 792 us; the launch traced here: 790 us
  waiting for transfers between devices  617 us (78%)
  local copies, waits for them, and re-layouts  79.1 us (10%)
  matrix products  63.9 us (8%)
  between operations  13.6 us (2%)
    ppermute x63, waiting for transfers between devices, from_behind(): lax.ppermute(value, axis, [(i, (i + by) % count) for i in range(count)])  410 us
    reduce_scatter x1, waiting for transfers between devices, per_device(): lax.psum_scatter(total + lax.dot_general(w_value, d_value, contract, pref...  146 us
    all_gather x1, waiting for transfers between devices, per_device(): lax.all_gather(out_grad, 'head', axis=1, tiled=True)  60.7 us
    broadcast_in_dim x31, local copies, waits for them, and re-layouts, visit(): jnp.repeat(jnp.repeat(listed, TILE, axis=0), TILE, axis=1)  49.5 us
    dynamic_slice x32, local copies, waits for them, and re-layouts, visit(): lax.dynamic_slice_in_dim(trace_id, first_tile * TILE, key_block.shape[0], 0)  24.4 us
  transfers between devices with their start and end apart: 65, of which 34 were waited for; matrix products, arithmetic and copies ran while one was open for 2% of the time, Pallas kernels for 0%

commit v1 on v0

--- a/solution.py
+++ b/solution.py
@@ -89,30 +89,21 @@
         )
         return pair_grads(query_heads, key_block, value_block, grad_heads, lse, delta, admit)
 
-    zero_rows = jnp.zeros((tokens_here, heads_here, HD), jnp.float32)
-
-    def pass_sums(sums):
-        return from_behind(sums, "seq", 1)
-
-    def cycle_work(step, held, sums, query_sum):
-        source = (seq_index - step) % seq_count
-        query_add, key_add, value_add = visit(held[0], held[1], source * tiles_here)
-        return (query_sum + query_add, sums + jnp.stack([settle(key_add), settle(value_add)]))
-
-    def cycle_turn(step, carry):
-        held, sums, query_sum = carry
-        query_sum, sums = cycle_work(step, held, sums, query_sum)
-        held = from_behind(held, "seq", 1)
-        return (held, pass_sums(sums), query_sum)
-
-    start_carry = (
-        jnp.stack([key_heads, value_heads]),
-        jnp.stack([zero_rows, zero_rows]),
-        zero_rows,
-    )
-    held, sums, query_sum = lax.fori_loop(0, seq_count - 1, cycle_turn, start_carry)
-    query_sum, sums = cycle_work(seq_count - 1, held, sums, query_sum)
-    sums = pass_sums(sums)
+    kv_all = lax.all_gather(jnp.stack([key_heads, value_heads]), "seq", axis=1, tiled=True)
+    total_tokens = kv_all.shape[1]
+    chunk = min(total_tokens, 2048)
+    query_sum = None
+    key_parts, value_parts = [], []
+    for first in range(0, total_tokens, chunk):
+        query_add, key_add, value_add = visit(
+            kv_all[0, first:first + chunk], kv_all[1, first:first + chunk], first // TILE
+        )
+        query_sum = query_add if query_sum is None else query_sum + query_add
+        key_parts.append(key_add)
+        value_parts.append(value_add)
+    parts = jnp.stack([jnp.concatenate(key_parts), jnp.concatenate(value_parts)])
+    parts = parts.astype(jnp.bfloat16).astype(jnp.float32)
+    sums = lax.psum_scatter(parts, "seq", scatter_dimension=1, tiled=True)
     key_sum, value_sum = (sums[0], sums[1])
     d_query = query_sum.astype(jnp.bfloat16).reshape(tokens_here, width)
     d_key = key_sum.astype(jnp.bfloat16).reshape(tokens_here, width)

time: 792 us -> 468 us (0.59)
  waiting for transfers between devices: 617 us -> 372 us
  local copies, waits for them, and re-layouts: 79.1 us -> 6.46 us
    ppermute x63 -> x0, waiting for transfers between devices: 410 us -> none  [from_behind(): lax.ppermute(value, axis, [(i, (i + by) % count) for i in range(count)])]
    reduce_scatter x0 -> x1, waiting for transfers between devices: none -> 134 us  [per_device(): sums = lax.psum_scatter(parts, 'seq', scatter_dimension=1, tiled=True)]
    all_gather x0 -> x1, waiting for transfers between devices: none -> 64.9 us  [per_device(): lax.all_gather(jnp.stack([key_heads, value_heads]), 'seq', axis=1, tiled=...]
    broadcast_in_dim x31 -> x0, local copies, waits for them, and re-layouts: 49.5 us -> none  [visit(): jnp.repeat(jnp.repeat(listed, TILE, axis=0), TILE, axis=1)]
    reduce_scatter x1, waiting for transfers between devices: 146 us -> 114 us  [per_device(): lax.psum_scatter(total + lax.dot_general(w_value, d_value, contract, pref...]
    dynamic_slice x32 -> x1, local copies, waits for them, and re-layouts: 24.4 us -> 0.82 us  [visit(): lax.dynamic_slice_in_dim(trace_id, first_tile * TILE, key_block.shape[0], 0)]
  transfers between devices with their start and end apart: 65 -> 4, of which waited for: 34 -> 4; matrix products, arithmetic and copies ran while one was open for 2% -> 5% of each run, Pallas kernels for 0% -> 0%
where the time goes in v1:
time: 468 us; the launch traced here: 466 us
  waiting for transfers between devices  372 us (79%)
  matrix products  60.5 us (13%)
  between operations  13.8 us (3%)
  other arithmetic  13.7 us (3%)
  local copies, waits for them, and re-layouts  6.46 us (1%)
    reduce_scatter x1, waiting for transfers between devices, per_device(): sums = lax.psum_scatter(parts, 'seq', scatter_dimension=1, tiled=True)  134 us
    reduce_scatter x1, waiting for transfers between devices, per_device(): lax.psum_scatter(total + lax.dot_general(w_value, d_value, contract, pref...  114 us
    all_gather x1, waiting for transfers between devices, per_device(): lax.all_gather(jnp.stack([key_heads, value_heads]), 'seq', axis=1, tiled=...  64.9 us
    all_gather x1, waiting for transfers between devices, per_device(): lax.all_gather(out_grad, 'head', axis=1, tiled=True)  58.1 us
    dot_general x8, matrix products, pair_grads(): jnp.einsum('rhd,chd->hrc', query_heads, key_heads, preferred_element_type...  12.6 us
    dot_general x8, matrix products, pair_grads(): jnp.einsum('hrc,rhd->chd', score_grad, query_heads, preferred_element_typ...  12.2 us
    dot_general x7, matrix products, pair_grads(): jnp.einsum('hrc,chd->rhd', score_grad, key_heads, preferred_element_type=...  12.1 us
  transfers between devices with their start and end apart: 4, of which 4 were waited for; matrix products, arithmetic and copies ran while one was open for 5% of the time, Pallas kernels for 0%

profile of v1, /device:TPU:32, one launch (start us, length us, event | category | flops | bytes accessed | tf_op | source)
XLA Modules:
  0.0 466.0 jit_solution(15415971764089354797)
XLA Ops:
  7.3 1.7 pad_maximum_fusion
  14.9 58.1 %all-gather.5.cloned.1.call-done = bf16[512,1024]{1,0:T(8,128)(2,1)} async-done(((bf16[512,128]{1,0:T(8,128)(2,1)}), bf16[512,1024]{1,0:T(8,128)(2,1)}) %all-gather.5.cloned.1.call-update) | async-done | bytes 1048592 | tf_op jit(solution)/shard_map/all_gather | solution.py:65
  73.0 1.8 multiply_reduce_fusion
  74.8 64.9 %all-gather.3.cloned.1.call-done = bf16[2,16384,1,128]{3,1,2,0:T(8,128)(2,1)} async-done(((bf16[2,512,1,128]{3,1,2,0:T(8,128)(2,1)}), bf16[2,16384,1,128]{3,1,2,0:T(8,128)(2,1)}) %all-gather.3.cloned.1.call-update) | async-done | bytes 8388624 | tf_op jit(solution)/shard_map/all_gather | solution.py:92
  139.7 2.7 bitcast_select_fusion.7
  144.1 1.6 fusion.1
  155.2 1.4 bitcast_select_fusion.2
  157.7 1.4 bitcast_select_fusion.1
  160.1 1.9 copy-done.17
  163.5 1.5 fusion.31
  165.7 1.5 fusion.3
  167.9 1.5 fusion.5
  170.1 1.5 fusion.7
  172.3 1.6 fusion.9
  174.6 1.5 fusion.11
  176.1 1.8 multiply_convert_fusion.1
  177.9 1.5 fusion.13
  179.5 2.1 multiply_convert_fusion
  181.6 1.5 fusion.15
  183.1 7.7 %maximum_convert_fusion = f32[2,16384,1,128]{3,1,2,0:T(8,128)} fusion(bf16[1,16384,1,128]{3,1,2,0:T(8,128)(2,1)S(1)} %bitcast.341, bf16[1,16384,1,128]{3,1,2,0:T(8,128)(2,1)} %bitcast.62), kind=kLoop, calls=%fused_computation | loop fusion | flops 8388608 | bytes 25165824 | tf_op jit(solution)/shard_map/convert_element_type | solution.py:105
  191.0 2.4 fusion.43
  193.4 1.7 convolution_add_fusion.6
  195.0 1.7 convolution_add_fusion.5
  196.7 1.7 convolution_add_fusion.4
  198.4 1.7 convolution_add_fusion.3
  200.1 1.5 convolution_add_fusion.2
  201.7 1.6 convolution_add_fusion.1
  203.3 3.4 fusion.42
  206.7 134.2 %reduce-scatter.3.cloned.1.call-done = f32[2,512,1,128]{3,1,2,0:T(8,128)} async-done(((f32[2,16384,1,128]{3,1,2,0:T(8,128)}), f32[2,512,1,128]{3,1,2,0:T(8,128)}) %reduce-scatter.3.cloned.1.call-update) | async-done | bytes 524304 | tf_op jit(solution)/shard_map/reduce_scatter | solution.py:106
  342.4 1.8 add_bitcast_fusion
  344.3 113.6 %reduce-scatter.5.cloned.1.call-done = f32[128,512]{0,1:T(8,128)} async-done(((f32[1024,512]{0,1:T(8,128)}), f32[128,512]{0,1:T(8,128)}) %reduce-scatter.5.cloned.1.call-update) | async-done | bytes 262160 | tf_op jit(solution)/shard_map/reduce_scatter | solution.py:114
  457.8 1.6 convert_bitcast_fusion
  (101 shorter events, 26.2 us)
Async XLA Ops:
  6.5 196.7 %copy-start = (bf16[1024,128]{1,0:T(8,128)(2,1)S(1)}, bf16[1024,128]{1,0:T(8,128)(2,1)}, u32[]{:S(2)}) copy-start(bf16[1024,128]{1,0:T(8,128)(2,1)} %param.22) | copy-start | bytes 786436
  6.5 66.5 %all-gather.5.cloned.1.call-start = ((), (), s32[]{:S(2)}) async-start(), calls=%async_computation.3 | async-start | bytes 1179648 | tf_op jit(solution)/shard_map/all_gather | solution.py:65
  7.3 132.5 %all-gather.3.cloned.1.call-start = ((), (), s32[]{:S(2)}) async-start(), calls=%async_computation.2 | async-start | bytes 8650752 | tf_op jit(solution)/shard_map/all_gather | solution.py:92
  9.0 331.8 %reduce-scatter.3.cloned.1.call-start = ((), (), s32[]{:S(2)}) async-start(), calls=%async_computation.4 | async-start | bytes 17301504 | tf_op jit(solution)/shard_map/reduce_scatter | solution.py:106
  139.7 3.6 copy-start.14
  143.2 1.0 copy-start.1
  143.3 2.3 copy-start.21
  144.1 3.9 copy-start.16
  160.1 1.9 copy-start.17
  167.9 2.2 copy-start.2
  170.1 2.3 copy-start.4
  172.3 2.3 copy-start.6
  174.6 3.3 copy-start.8
  177.9 3.7 copy-start.10
  179.4 3.7 copy-start.18
  181.6 1.5 copy-start.12
  190.9 266.9 %reduce-scatter.5.cloned.1.call-start = ((), (), s32[]{:S(2)}) async-start(), calls=%async_computation.5 | async-start | bytes 2359296 | tf_op jit(solution)/shard_map/reduce_scatter | solution.py:114
  191.0 4.1 copy-start.3
  191.0 5.8 %copy-start.5 = (bf16[512,2048]{0,1:T(8,128)(2,1)S(1)}, bf16[512,2048]{0,1:T(8,128)(2,1)}, u32[]{:S(2)}) copy-start(bf16[512,2048]{0,1:T(8,128)(2,1)} %copy-done.4) | copy-start | bytes 6291460
  193.3 5.1 %copy-start.7 = (bf16[512,2048]{0,1:T(8,128)(2,1)S(1)}, bf16[512,2048]{0,1:T(8,128)(2,1)}, u32[]{:S(2)}) copy-start(bf16[512,2048]{0,1:T(8,128)(2,1)} %copy-done.6) | copy-start | bytes 6291460
  195.0 5.1 %copy-start.9 = (bf16[512,2048]{0,1:T(8,128)(2,1)S(1)}, bf16[512,2048]{0,1:T(8,128)(2,1)}, u32[]{:S(2)}) copy-start(bf16[512,2048]{0,1:T(8,128)(2,1)} %copy-done.8) | copy-start | bytes 6291460
  196.7 4.9 %copy-start.11 = (bf16[512,2048]{0,1:T(8,128)(2,1)S(1)}, bf16[512,2048]{0,1:T(8,128)(2,1)}, u32[]{:S(2)}) copy-start(bf16[512,2048]{0,1:T(8,128)(2,1)} %copy-done.10) | copy-start | bytes 6291460
  198.4 4.8 %copy-start.13 = (bf16[512,2048]{0,1:T(8,128)(2,1)S(1)}, bf16[512,2048]{0,1:T(8,128)(2,1)}, u32[]{:S(2)}) copy-start(bf16[512,2048]{0,1:T(8,128)(2,1)} %copy-done.12) | copy-start | bytes 6291460
  201.6 140.3 %copy-start.19 = (bf16[1024,128]{1,0:T(8,128)(2,1)S(1)}, bf16[1024,128]{1,0:T(8,128)(2,1)}, u32[]{:S(2)}) copy-start(bf16[1024,128]{1,0:T(8,128)(2,1)} %param.23) | copy-start | bytes 786436
  203.2 139.1 %copy-start.20 = (bf16[1024,128]{1,0:T(8,128)(2,1)S(1)}, bf16[1024,128]{1,0:T(8,128)(2,1)}, u32[]{:S(2)}) copy-start(bf16[1024,128]{1,0:T(8,128)(2,1)} %param.24) | copy-start | bytes 786436
  206.7 135.7 %copy-start.15 = (f32[512,1024]{1,0:T(8,128)S(1)}, f32[512,1024]{1,0:T(8,128)}, u32[]{:S(2)}) copy-start(f32[512,1024]{1,0:T(8,128)} %fusion.42) | copy-start | bytes 6291460
Sparse Core Ops, SparseCore 0:
  9.8 63.1 all-gather.4
  74.9 64.7 all-gather.2
  191.0 149.7 reduce-scatter.2
  344.8 113.0 reduce-scatter.4

commit v2 on v1

--- a/solution.py
+++ b/solution.py
@@ -61,9 +61,17 @@
     seq_count = lax.axis_size("seq")
     seq_index = lax.axis_index("seq")
     tiles_here = tokens_here // TILE
+    head_count = lax.axis_size("head")
+    head_index = lax.axis_index("head")
+    grad_blocks = [out_grad] + [from_behind(out_grad, "head", shift) for shift in range(1, head_count)]
+    block_order = (head_index - jnp.arange(head_count)) % head_count
+    block_width = out_grad.shape[1]
+    w_out_blocks = jnp.take(
+        w_out.reshape(w_out.shape[0], head_count, block_width), block_order, axis=1
+    ).reshape(w_out.shape[0], head_count * block_width)
     d_attn = lax.dot_general(
-        lax.all_gather(out_grad, "head", axis=1, tiled=True),
-        w_out,
+        jnp.concatenate(grad_blocks, axis=1),
+        w_out_blocks,
         (((1,), (1,)), ((), ())),
         preferred_element_type=jnp.float32,
     ).astype(jnp.bfloat16)
@@ -102,8 +110,8 @@
         key_parts.append(key_add)
         value_parts.append(value_add)
     parts = jnp.stack([jnp.concatenate(key_parts), jnp.concatenate(value_parts)])
-    parts = parts.astype(jnp.bfloat16).astype(jnp.float32)
-    sums = lax.psum_scatter(parts, "seq", scatter_dimension=1, tiled=True)
+    parts = parts.astype(jnp.bfloat16).reshape((2, seq_count, tokens_here) + parts.shape[2:])
+    sums = lax.all_to_all(parts, "seq", 1, 1, tiled=False).astype(jnp.float32).sum(axis=1)
     key_sum, value_sum = (sums[0], sums[1])
     d_query = query_sum.astype(jnp.bfloat16).reshape(tokens_here, width)
     d_key = key_sum.astype(jnp.bfloat16).reshape(tokens_here, width)
@@ -111,12 +119,9 @@
     contract = (((1,), (1,)), ((), ()))
     total = lax.dot_general(w_query, d_query, contract, preferred_element_type=jnp.float32)
     total = total + lax.dot_general(w_key, d_key, contract, preferred_element_type=jnp.float32)
-    d_input = lax.psum_scatter(
-        total + lax.dot_general(w_value, d_value, contract, preferred_element_type=jnp.float32),
-        "head",
-        scatter_dimension=0,
-        tiled=True,
-    )
+    total = total + lax.dot_general(w_value, d_value, contract, preferred_element_type=jnp.float32)
+    total = total.reshape((head_count, total.shape[0] // head_count) + total.shape[1:])
+    d_input = lax.all_to_all(total, "head", 0, 0, tiled=False).sum(axis=0)
     return d_input.T.astype(jnp.bfloat16)
 
 

time: 468 us -> 437 us (0.934); the launches traced: 466 us -> 430 us
  waiting for transfers between devices: 372 us -> 219 us
  blocking collectives: 0 us -> 56.4 us
  starting transfers between devices: 0.12 us -> 26.5 us
  matrix products: 60.5 us -> 76.9 us
  local copies, waits for them, and re-layouts: 6.46 us -> 19.9 us
    reduce_scatter x2 -> x0, waiting for transfers between devices: 248 us -> none  [the longest x1 134 us: per_device(): sums = lax.psum_scatter(parts, 'seq', scatter_dimension=1, tiled=True)]
    all_to_all x0 -> x1, waiting for transfers between devices: none -> 167 us  [per_device(): lax.all_to_all(parts, 'seq', 1, 1, tiled=False).astype(jnp.float32)]
    all_gather x1 -> x0, waiting for transfers between devices: 58.1 us -> none  [per_device(): lax.all_gather(out_grad, 'head', axis=1, tiled=True)]
    all_to_all x0 -> x1, blocking collectives: none -> 56.4 us  [per_device(): d_input = lax.all_to_all(total, 'head', 0, 0, tiled=False).sum(axis=0)]
    all_gather x1, waiting for transfers between devices: 64.9 us -> 38.2 us  [per_device(): lax.all_gather(jnp.stack([key_heads, value_heads]), 'seq', axis=1, tiled=...]
    ppermute x0 -> x7, starting transfers between devices: none -> 20.7 us  [from_behind(): lax.ppermute(value, axis, [(i, (i + by) % count) for i in range(count)])]
    ppermute x0 -> x7, waiting for transfers between devices: none -> 14 us  [from_behind(): lax.ppermute(value, axis, [(i, (i + by) % count) for i in range(count)])]
    convert_element_type x2 -> x0, other arithmetic: 9.36 us -> none  [the longest x1 7.75 us: per_device(): parts = parts.astype(jnp.bfloat16).astype(jnp.float32)]
  transfers between devices with their start and end apart: 4 -> 9, of which waited for: 4 -> 5; matrix products, arithmetic and copies ran while one was open for 5% -> 6% of each run, Pallas kernels for 0% -> 0%
where the time goes in v2:
time: 437 us; the launch traced here: 430 us
  waiting for transfers between devices  219 us (50%)
  matrix products  76.9 us (18%)
  blocking collectives  56.4 us (13%)
  starting transfers between devices  26.5 us (6%)
  local copies, waits for them, and re-layouts  19.9 us (5%)
  other arithmetic  16.7 us (4%)
  between operations  14.4 us (3%)
    all_to_all x1, waiting for transfers between devices, per_device(): lax.all_to_all(parts, 'seq', 1, 1, tiled=False).astype(jnp.float32)  167 us
    all_to_all x1, blocking collectives, per_device(): d_input = lax.all_to_all(total, 'head', 0, 0, tiled=False).sum(axis=0)  56.4 us
    all_gather x1, waiting for transfers between devices, per_device(): lax.all_gather(jnp.stack([key_heads, value_heads]), 'seq', axis=1, tiled=...  38.2 us
    ppermute x7, starting transfers between devices, from_behind(): lax.ppermute(value, axis, [(i, (i + by) % count) for i in range(count)])  20.7 us
    dot_general x8, matrix products, pair_grads(): jnp.einsum('rhd,chd->hrc', query_heads, key_heads, preferred_element_type...  20.3 us
    dot_general x8, matrix products, pair_grads(): jnp.einsum('hrc,rhd->chd', probs.astype(jnp.bfloat16), grad_heads, prefer...  16.4 us
    dot_general x8, matrix products, pair_grads(): jnp.einsum('rhd,chd->hrc', grad_heads, value_heads, preferred_element_typ...  16.3 us
    ppermute x7, waiting for transfers between devices, from_behind(): lax.ppermute(value, axis, [(i, (i + by) % count) for i in range(count)])  14 us
  transfers between devices with their start and end apart: 9, of which 5 were waited for; matrix products, arithmetic and copies ran while one was open for 6% of the time, Pallas kernels for 0%

profile of v2, /device:TPU:32, one launch (start us, length us, event | category | flops | bytes accessed | tf_op | source)
XLA Modules:
  0.0 429.8 jit_solution(8207958485833883073)
XLA Ops:
  8.4 6.4 %collective-permute-start = (bf16[512,128]{1,0:T(8,128)(2,1)}, bf16[512,128]{1,0:T(8,128)(2,1)S(1)}, u32[]{:S(2)}, u32[]{:S(2)}) collective-permute-start(bf16[512,128]{1,0:T(8,128)(2,1)} %param.17), channel_id=1, source_target_pairs={{0,1},{1,2},{2,3},{3,4},{4,5},{5,6},{6,7},{7,0},{8,9},{9,10},{10,1... | collective-permute-start | bytes 393224 | tf_op jit(solution)/shard_map/ppermute | solution.py:13
  17.4 2.0 collective-permute-start.3
  19.4 7.9 %collective-permute-start.4 = (bf16[512,128]{1,0:T(8,128)(2,1)}, bf16[512,128]{1,0:T(8,128)(2,1)S(1)}, u32[]{:S(2)}, u32[]{:S(2)}) collective-permute-start(bf16[512,128]{1,0:T(8,128)(2,1)} %param.17), channel_id=1, source_target_pairs={{0,5},{1,6},{2,7},{3,0},{4,1},{5,2},{6,3},{7,4},{8,13},{9,14},{10,... | collective-permute-start | bytes 393224 | tf_op jit(solution)/shard_map/ppermute | solution.py:13
  41.7 10.9 %collective-permute-done.6 = bf16[512,128]{1,0:T(8,128)(2,1)S(1)} collective-permute-done((bf16[512,128]{1,0:T(8,128)(2,1)S(1)}, bf16[512,128]{1,0:T(8,128)(2,1)S(1)}, u32[]{:S(2)}, u32[]{:S(2)}) %collective-permute-start.6) | collective-permute-done | bytes 131104 | tf_op jit(solution)/shard_map/ppermute | solution.py:13
  53.1 38.2 %all-gather.2.cloned.1.call-done = bf16[2,16384,1,128]{3,1,2,0:T(8,128)(2,1)} async-done(((bf16[2,512,1,128]{3,1,2,0:T(8,128)(2,1)}), bf16[2,16384,1,128]{3,1,2,0:T(8,128)(2,1)}) %all-gather.2.cloned.1.call-update) | async-done | bytes 8388624 | tf_op jit(solution)/shard_map/all_gather | solution.py:100
  91.4 2.5 bitcast_select_fusion.7
  93.9 2.1 fusion.17
  96.1 2.5 bitcast_select_fusion.6
  98.6 2.1 fusion.19
  100.7 2.5 bitcast_select_fusion.5
  103.2 2.1 fusion.21
  105.3 2.5 bitcast_select_fusion.4
  107.9 2.1 fusion.23
  110.0 2.5 bitcast_select_fusion.3
  112.6 2.1 fusion.25
  114.7 2.5 bitcast_select_fusion.2
  117.3 2.2 fusion.27
  119.4 2.5 bitcast_select_fusion.1
  122.0 2.1 fusion.29
  124.1 2.5 bitcast_select_fusion
  126.7 2.0 copy-done.14
  130.3 6.4 %copy.93 = bf16[16384,1,128]{2,0,1:T(8,128)(2,1)} copy(bf16[16384,1,128]{0,2,1:T(8,128)(2,1)} %fusion.31) | data formatting | bytes 8388608 | tf_op jit(solution)/shard_map/stack | solution.py:112
  136.6 3.2 multiply_convert_fusion.7
  141.9 1.9 multiply_convert_fusion.6
  162.1 2.0 copy-done.31
  164.1 7.6 %pad_maximum_fusion = bf16[2,32,512,1,128]{4,2,3,0,1:T(8,128)(2,1)} fusion(bf16[1,32,512,1,128]{4,2,3,0,1:T(8,128)(2,1)} %bitcast.356, bf16[1,32,512,1,128]{4,2,3,0,1:T(8,128)(2,1)} %bitcast.358), kind=kLoop, calls=%fused_computation.1 | loop fusion | flops 4194304 | bytes 16777216 | tf_op jit(solution)/shard_map/stack | solution.py:112
  171.7 5.8 %all-to-all-start = ((bf16[2,32,512,1,128]{4,2,3,0,1:T(8,128)(2,1)}), bf16[2,32,512,1,128]{4,2,3,0,1:T(8,128)(2,1)}, u32[]{:S(2)}, u32[]{:S(2)}) async-start(bf16[2,32,512,1,128]{4,2,3,0,1:T(8,128)(2,1)} %pad_maximum_fusion), calls=%async_computation | async-start | bytes 16777216 | tf_op jit(solution)/shard_map/all_to_all | solution.py:114
  177.5 2.4 fusion.43
  189.7 3.3 fusion.42
  193.1 166.8 %all-to-all-done = bf16[2,32,512,1,128]{4,2,3,0,1:T(8,128)(2,1)} async-done(((bf16[2,32,512,1,128]{4,2,3,0,1:T(8,128)(2,1)}), bf16[2,32,512,1,128]{4,2,3,0,1:T(8,128)(2,1)}, u32[]{:S(2)}, u32[]{:S(2)}) %all-to-all-start) | async-done | bytes 8388640 | tf_op jit(solution)/shard_map/all_to_all | solution.py:114
  359.8 4.8 %reduce.3 = bf16[2,512,128]{2,1,0:T(8,128)(2,1)S(1)} reduce(bf16[2,32,512,1,128]{4,2,3,0,1:T(8,128)(2,1)} %all-to-all-done, bf16[]{:T(256)} %constant.53), dimensions={1,3}, to_apply=%region_2.3.clone | reduce | flops 4063232 | bytes 8650754 | tf_op jit(solution)/shard_map/reduce_sum | solution.py:114
  365.7 56.4 %all_to_all.10 = f32[8,128,512]{1,2,0:T(8,128)S(1)} all-to-all(f32[8,128,512]{1,2,0:T(8,128)S(1)} %bitcast.357), channel_id=1, replica_groups=mesh['seq'=32,'head'=8] {'head'}, dimensions={0} | all-to-all | bytes 4194304 | tf_op jit(solution)/shard_map/all_to_all | solution.py:124
  (156 shorter events, 52.4 us)
Async XLA Ops:
  6.5 183.2 %copy-start = (bf16[1024,128]{1,0:T(8,128)(2,1)S(1)}, bf16[1024,128]{1,0:T(8,128)(2,1)}, u32[]{:S(2)}) copy-start(bf16[1024,128]{1,0:T(8,128)(2,1)} %param.22) | copy-start | bytes 786436
  6.5 30.0 %copy-start.35 = (bf16[512,128]{1,0:T(8,128)(2,1)S(1)}, bf16[512,128]{1,0:T(8,128)(2,1)}, u32[]{:S(2)}) copy-start(bf16[512,128]{1,0:T(8,128)(2,1)} %param.17) | copy-start | bytes 393220
  6.5 84.8 %copy-start.16 = (bf16[512,128]{1,0:T(8,128)(2,1)S(1)}, bf16[512,128]{1,0:T(8,128)(2,1)}, u32[]{:S(2)}) copy-start(bf16[512,128]{1,0:T(8,128)(2,1)} %param.13) | copy-start | bytes 393220
  6.5 84.8 %copy-start.34 = (f32[1,512]{1,0:T(1,128)S(1)}, f32[1,512]{1,0:T(1,128)}, u32[]{:S(2)}) copy-start(f32[1,512]{1,0:T(1,128)} %param.18) | copy-start | bytes 6148
  6.5 84.8 %all-gather.2.cloned.1.call-start = ((), (), s32[]{:S(2)}) async-start(), calls=%async_computation.2 | async-start | bytes 8650752 | tf_op jit(solution)/shard_map/all_gather | solution.py:100
  8.4 28.2 %collective-permute-start = (bf16[512,128]{1,0:T(8,128)(2,1)}, bf16[512,128]{1,0:T(8,128)(2,1)S(1)}, u32[]{:S(2)}, u32[]{:S(2)}) collective-permute-start(bf16[512,128]{1,0:T(8,128)(2,1)} %param.17), channel_id=1, source_target_pairs={{0,1},{1,2},{2,3},{3,4},{4,5},{5,6},{6,7},{7,0},{8,9},{9,10},{10,1... | collective-permute-start | bytes 393224 | tf_op jit(solution)/shard_map/ppermute | solution.py:13
  14.7 23.4 %collective-permute-start.1 = (bf16[512,128]{1,0:T(8,128)(2,1)}, bf16[512,128]{1,0:T(8,128)(2,1)S(1)}, u32[]{:S(2)}, u32[]{:S(2)}) collective-permute-start(bf16[512,128]{1,0:T(8,128)(2,1)} %param.17), channel_id=1, source_target_pairs={{0,2},{1,3},{2,4},{3,5},{4,6},{5,7},{6,0},{7,1},{8,10},{9,11},{10,... | collective-permute-start | bytes 393224 | tf_op jit(solution)/shard_map/ppermute | solution.py:13
  16.2 22.2 %collective-permute-start.2 = (bf16[512,128]{1,0:T(8,128)(2,1)}, bf16[512,128]{1,0:T(8,128)(2,1)S(1)}, u32[]{:S(2)}, u32[]{:S(2)}) collective-permute-start(bf16[512,128]{1,0:T(8,128)(2,1)} %param.17), channel_id=1, source_target_pairs={{0,3},{1,4},{2,5},{3,6},{4,7},{5,0},{6,1},{7,2},{8,11},{9,12},{10,... | collective-permute-start | bytes 393224 | tf_op jit(solution)/shard_map/ppermute | solution.py:13
  17.4 21.1 %collective-permute-start.3 = (bf16[512,128]{1,0:T(8,128)(2,1)}, bf16[512,128]{1,0:T(8,128)(2,1)S(1)}, u32[]{:S(2)}, u32[]{:S(2)}) collective-permute-start(bf16[512,128]{1,0:T(8,128)(2,1)} %param.17), channel_id=1, source_target_pairs={{0,4},{1,5},{2,6},{3,7},{4,0},{5,1},{6,2},{7,3},{8,12},{9,13},{10,... | collective-permute-start | bytes 393224 | tf_op jit(solution)/shard_map/ppermute | solution.py:13
  19.4 20.5 %collective-permute-start.4 = (bf16[512,128]{1,0:T(8,128)(2,1)}, bf16[512,128]{1,0:T(8,128)(2,1)S(1)}, u32[]{:S(2)}, u32[]{:S(2)}) collective-permute-start(bf16[512,128]{1,0:T(8,128)(2,1)} %param.17), channel_id=1, source_target_pairs={{0,5},{1,6},{2,7},{3,0},{4,1},{5,2},{6,3},{7,4},{8,13},{9,14},{10,... | collective-permute-start | bytes 393224 | tf_op jit(solution)/shard_map/ppermute | solution.py:13
  36.6 5.0 %collective-permute-start.5 = (bf16[512,128]{1,0:T(8,128)(2,1)S(1)}, bf16[512,128]{1,0:T(8,128)(2,1)S(1)}, u32[]{:S(2)}, u32[]{:S(2)}) collective-permute-start(bf16[512,128]{1,0:T(8,128)(2,1)S(1)} %copy-done.35), channel_id=1, source_target_pairs={{0,6},{1,7},{2,0},{3,1},{4,2},{5,3},{6,4},{7,5},{8,14},{9,15},{10,... | collective-permute-start | bytes 393224 | tf_op jit(solution)/shard_map/ppermute | solution.py:13
  38.1 14.5 %collective-permute-start.6 = (bf16[512,128]{1,0:T(8,128)(2,1)S(1)}, bf16[512,128]{1,0:T(8,128)(2,1)S(1)}, u32[]{:S(2)}, u32[]{:S(2)}) collective-permute-start(bf16[512,128]{1,0:T(8,128)(2,1)S(1)} %copy-done.35), channel_id=1, source_target_pairs={{0,7},{1,0},{2,1},{3,2},{4,3},{5,4},{6,5},{7,6},{8,15},{9,8},{10,9... | collective-permute-start | bytes 393224 | tf_op jit(solution)/shard_map/ppermute | solution.py:13
  93.9 4.7 %copy-start.1 = (f32[512,2048]{0,1:T(8,128)}, f32[512,2048]{0,1:T(8,128)S(1)}, u32[]{:S(2)}) copy-start(f32[512,2048]{0,1:T(8,128)S(1)} %bitcast_select_fusion.7) | copy-start | bytes 12582916
  98.6 4.6 %copy-start.2 = (f32[512,2048]{0,1:T(8,128)}, f32[512,2048]{0,1:T(8,128)S(1)}, u32[]{:S(2)}) copy-start(f32[512,2048]{0,1:T(8,128)S(1)} %bitcast_select_fusion.6) | copy-start | bytes 12582916
  103.2 4.6 %copy-start.4 = (f32[512,2048]{0,1:T(8,128)}, f32[512,2048]{0,1:T(8,128)S(1)}, u32[]{:S(2)}) copy-start(f32[512,2048]{0,1:T(8,128)S(1)} %bitcast_select_fusion.5) | copy-start | bytes 12582916
  107.9 4.7 %copy-start.6 = (f32[512,2048]{0,1:T(8,128)}, f32[512,2048]{0,1:T(8,128)S(1)}, u32[]{:S(2)}) copy-start(f32[512,2048]{0,1:T(8,128)S(1)} %bitcast_select_fusion.4) | copy-start | bytes 12582916
  112.6 4.6 %copy-start.8 = (f32[512,2048]{0,1:T(8,128)}, f32[512,2048]{0,1:T(8,128)S(1)}, u32[]{:S(2)}) copy-start(f32[512,2048]{0,1:T(8,128)S(1)} %bitcast_select_fusion.3) | copy-start | bytes 12582916
  117.2 4.7 %copy-start.10 = (f32[512,2048]{0,1:T(8,128)}, f32[512,2048]{0,1:T(8,128)S(1)}, u32[]{:S(2)}) copy-start(f32[512,2048]{0,1:T(8,128)S(1)} %bitcast_select_fusion.2) | copy-start | bytes 12582916
  122.0 4.7 %copy-start.12 = (f32[512,2048]{0,1:T(8,128)}, f32[512,2048]{0,1:T(8,128)S(1)}, u32[]{:S(2)}) copy-start(f32[512,2048]{0,1:T(8,128)S(1)} %bitcast_select_fusion.1) | copy-start | bytes 12582916
  136.6 5.3 %copy-start.3 = (f32[512,2048]{0,1:T(8,128)S(1)}, f32[512,2048]{0,1:T(8,128)}, u32[]{:S(2)}) copy-start(f32[512,2048]{0,1:T(8,128)} %copy-done.2) | copy-start | bytes 12582916
  147.6 2.9 copy-start.9
  150.5 2.9 copy-start.11
  171.7 188.1 %all-to-all-start = ((bf16[2,32,512,1,128]{4,2,3,0,1:T(8,128)(2,1)}), bf16[2,32,512,1,128]{4,2,3,0,1:T(8,128)(2,1)}, u32[]{:S(2)}, u32[]{:S(2)}) async-start(bf16[2,32,512,1,128]{4,2,3,0,1:T(8,128)(2,1)} %pad_maximum_fusion), calls=%async_computation | async-start | bytes 16777216 | tf_op jit(solution)/shard_map/all_to_all | solution.py:114
  177.5 4.1 copy-start.18
  177.5 5.8 %copy-start.20 = (bf16[512,2048]{0,1:T(8,128)(2,1)S(1)}, bf16[512,2048]{0,1:T(8,128)(2,1)}, u32[]{:S(2)}) copy-start(bf16[512,2048]{0,1:T(8,128)(2,1)} %copy-done.19) | copy-start | bytes 6291460
  179.9 5.1 %copy-start.22 = (bf16[512,2048]{0,1:T(8,128)(2,1)S(1)}, bf16[512,2048]{0,1:T(8,128)(2,1)}, u32[]{:S(2)}) copy-start(bf16[512,2048]{0,1:T(8,128)(2,1)} %copy-done.21) | copy-start | bytes 6291460
  181.6 5.1 %copy-start.24 = (bf16[512,2048]{0,1:T(8,128)(2,1)S(1)}, bf16[512,2048]{0,1:T(8,128)(2,1)}, u32[]{:S(2)}) copy-start(bf16[512,2048]{0,1:T(8,128)(2,1)} %copy-done.23) | copy-start | bytes 6291460
  183.3 4.9 %copy-start.26 = (bf16[512,2048]{0,1:T(8,128)(2,1)S(1)}, bf16[512,2048]{0,1:T(8,128)(2,1)}, u32[]{:S(2)}) copy-start(bf16[512,2048]{0,1:T(8,128)(2,1)} %copy-done.25) | copy-start | bytes 6291460
  185.0 4.8 %copy-start.28 = (bf16[512,2048]{0,1:T(8,128)(2,1)S(1)}, bf16[512,2048]{0,1:T(8,128)(2,1)}, u32[]{:S(2)}) copy-start(bf16[512,2048]{0,1:T(8,128)(2,1)} %copy-done.27) | copy-start | bytes 6291460
  193.1 171.6 %copy-start.32 = (bf16[1024,128]{1,0:T(8,128)(2,1)S(1)}, bf16[1024,128]{1,0:T(8,128)(2,1)}, u32[]{:S(2)}) copy-start(bf16[1024,128]{1,0:T(8,128)(2,1)} %param.23) | copy-start | bytes 786436
  193.1 172.0 %copy-start.29 = (f32[512,1024]{1,0:T(8,128)S(1)}, f32[512,1024]{1,0:T(8,128)}, u32[]{:S(2)}) copy-start(f32[512,1024]{1,0:T(8,128)} %fusion.42) | copy-start | bytes 6291460
  193.1 172.0 %copy-start.33 = (bf16[1024,128]{1,0:T(8,128)(2,1)S(1)}, bf16[1024,128]{1,0:T(8,128)(2,1)}, u32[]{:S(2)}) copy-start(bf16[1024,128]{1,0:T(8,128)(2,1)} %param.24) | copy-start | bytes 786436
  (13 other events, 32.1 us)
Sparse Core Ops, SparseCore 0:
  9.2 82.0 all-gather.1

commit v3 on v2

--- a/solution.py
+++ b/solution.py
@@ -88,31 +88,43 @@
         (key_tiles[:, :, None] == tile_range[None, None, :]) & slots[:, :, None], axis=1
     )
 
-    def visit(key_block, value_block, first_tile):
-        block_tiles = key_block.shape[0] // TILE
-        listed = lax.dynamic_slice(allowed, (0, first_tile), (tiles_here, block_tiles))
-        trace_keys = lax.dynamic_slice_in_dim(trace_id, first_tile * TILE, key_block.shape[0], 0)
-        admit = jnp.repeat(jnp.repeat(listed, TILE, axis=0), TILE, axis=1) & (
-            trace_here[:, None] != trace_keys[None, :]
+    kv_all = lax.all_gather(jnp.stack([key_heads, value_heads]), "seq", axis=1, tiled=True)
+    tile_total = kv_all.shape[1] // TILE
+    kv_tiles = kv_all.reshape((2, tile_total, TILE) + kv_all.shape[2:])
+    trace_tiles = trace_id.reshape(tile_total, TILE)
+    tile_ids = jnp.arange(tile_total)
+    query_rows = []
+    key_sum = None
+    value_sum = None
+    for row in range(tiles_here):
+        rows = slice(row * TILE, (row + 1) * TILE)
+        listed = key_tiles[row]
+        key_block = kv_tiles[0][listed].reshape((SEL * TILE,) + kv_all.shape[2:])
+        value_block = kv_tiles[1][listed].reshape((SEL * TILE,) + kv_all.shape[2:])
+        used = jnp.repeat(jnp.arange(SEL) < tile_count[row], TILE)
+        admit = used[None, :] & (trace_here[rows, None] != trace_tiles[listed].reshape(-1)[None, :])
+        query_add, key_add, value_add = pair_grads(
+            query_heads[rows], key_block, value_block, grad_heads[rows],
+            lse[:, rows], delta[:, rows], admit,
         )
-        return pair_grads(query_heads, key_block, value_block, grad_heads, lse, delta, admit)
-
-    kv_all = lax.all_gather(jnp.stack([key_heads, value_heads]), "seq", axis=1, tiled=True)
-    total_tokens = kv_all.shape[1]
-    chunk = min(total_tokens, 2048)
-    query_sum = None
-    key_parts, value_parts = [], []
-    for first in range(0, total_tokens, chunk):
-        query_add, key_add, value_add = visit(
-            kv_all[0, first:first + chunk], kv_all[1, first:first + chunk], first // TILE
+        query_rows.append(query_add)
+        onehot = (listed[:, None] == tile_ids[None, :]).astype(jnp.bfloat16)
+        spread = (((0,), (0,)), ((), ()))
+        key_add = lax.dot_general(
+            onehot, key_add.reshape((SEL, -1)).astype(jnp.bfloat16), spread,
+            preferred_element_type=jnp.float32,
         )
-        query_sum = query_add if query_sum is None else query_sum + query_add
-        key_parts.append(key_add)
-        value_parts.append(value_add)
-    parts = jnp.stack([jnp.concatenate(key_parts), jnp.concatenate(value_parts)])
-    parts = parts.astype(jnp.bfloat16).reshape((2, seq_count, tokens_here) + parts.shape[2:])
-    sums = lax.all_to_all(parts, "seq", 1, 1, tiled=False).astype(jnp.float32).sum(axis=1)
-    key_sum, value_sum = (sums[0], sums[1])
+        value_add = lax.dot_general(
+            onehot, value_add.reshape((SEL, -1)).astype(jnp.bfloat16), spread,
+            preferred_element_type=jnp.float32,
+        )
+        key_sum = key_add if key_sum is None else key_sum + key_add
+        value_sum = value_add if value_sum is None else value_sum + value_add
+    query_sum = jnp.concatenate(query_rows)
+    part_shape = (seq_count * tokens_here,) + kv_all.shape[2:]
+    key_sum = lax.psum_scatter(key_sum.reshape(part_shape), "seq", scatter_dimension=0, tiled=True)
+    value_parts = value_sum.astype(jnp.bfloat16).reshape((seq_count, tokens_here) + kv_all.shape[2:])
+    value_sum = lax.all_to_all(value_parts, "seq", 0, 0, tiled=False).astype(jnp.float32).sum(axis=0)
     d_query = query_sum.astype(jnp.bfloat16).reshape(tokens_here, width)
     d_key = key_sum.astype(jnp.bfloat16).reshape(tokens_here, width)
     d_value = value_sum.astype(jnp.bfloat16).reshape(tokens_here, width)

time: 437 us -> 469 us (1.073)
  the two profiles are of different devices: /device:TPU:32 before, /device:TPU:96 now
where the time goes in v3:
time: 469 us; the launch traced here: 461 us
  waiting for transfers between devices  163 us (35%)
  local copies, waits for them, and re-layouts  115 us (25%)
  matrix products  75.1 us (16%)
  blocking collectives  59.3 us (13%)
  starting transfers between devices  25.4 us (5%)
  between operations  14.6 us (3%)
  other arithmetic  8.21 us (2%)
    all_to_all x1, waiting for transfers between devices, per_device(): lax.all_to_all(value_parts, 'seq', 0, 0, tiled=False).astype(jnp.float32)  114 us
    all_to_all x1, blocking collectives, per_device(): d_input = lax.all_to_all(total, 'head', 0, 0, tiled=False).sum(axis=0)  59.3 us
    all_gather x1, waiting for transfers between devices, per_device(): lax.all_gather(jnp.stack([key_heads, value_heads]), 'seq', axis=1, tiled=...  31.9 us
    convert_element_type x8, local copies, waits for them, and re-layouts, per_device(): value_add.reshape((SEL, -1)).astype(jnp.bfloat16)  25.5 us
    dot_general x4, matrix products, pair_grads(): jnp.einsum('rhd,chd->hrc', query_heads, key_heads, preferred_element_type...  23 us
    ppermute x7, starting transfers between devices, from_behind(): lax.ppermute(value, axis, [(i, (i + by) % count) for i in range(count)])  18.7 us
    ppermute x7, waiting for transfers between devices, from_behind(): lax.ppermute(value, axis, [(i, (i + by) % count) for i in range(count)])  17.6 us
    gather x4, local copies, waits for them, and re-layouts, per_device(): key_block = kv_tiles[0][listed].reshape((SEL * TILE,) + kv_all.shape[2:])  16 us
  transfers between devices with their start and end apart: 10, of which 5 were waited for; matrix products, arithmetic and copies ran while one was open for 17% of the time, Pallas kernels for 0%

profile of v3, /device:TPU:96, one launch (start us, length us, event | category | flops | bytes accessed | tf_op | source)
XLA Modules:
  0.0 460.9 jit_solution(10201289074201295982)
XLA Ops:
  11.3 4.7 %collective-permute-start.4 = (bf16[512,128]{1,0:T(8,128)(2,1)}, bf16[512,128]{1,0:T(8,128)(2,1)S(1)}, u32[]{:S(2)}, u32[]{:S(2)}) collective-permute-start(bf16[512,128]{1,0:T(8,128)(2,1)} %param.17), channel_id=1, source_target_pairs={{0,5},{1,6},{2,7},{3,0},{4,1},{5,2},{6,3},{7,4},{8,13},{9,14},{10,... | collective-permute-start | bytes 393224 | tf_op jit(solution)/shard_map/ppermute | solution.py:13
  34.9 5.5 %collective-permute-start.2 = (bf16[512,128]{1,0:T(8,128)(2,1)S(1)}, bf16[512,128]{1,0:T(8,128)(2,1)S(1)}, u32[]{:S(2)}, u32[]{:S(2)}) collective-permute-start(bf16[512,128]{1,0:T(8,128)(2,1)S(1)} %copy-done.26), channel_id=1, source_target_pairs={{0,3},{1,4},{2,5},{3,6},{4,7},{5,0},{6,1},{7,2},{8,11},{9,12},{10,... | collective-permute-start | bytes 393224 | tf_op jit(solution)/shard_map/ppermute | solution.py:13
  43.3 9.2 %collective-permute-done.2 = bf16[512,128]{1,0:T(8,128)(2,1)S(1)} collective-permute-done((bf16[512,128]{1,0:T(8,128)(2,1)S(1)}, bf16[512,128]{1,0:T(8,128)(2,1)S(1)}, u32[]{:S(2)}, u32[]{:S(2)}) %collective-permute-start.2) | collective-permute-done | bytes 131104 | tf_op jit(solution)/shard_map/ppermute | solution.py:13
  52.7 6.9 %collective-permute-done.6 = bf16[512,128]{1,0:T(8,128)(2,1)S(1)} collective-permute-done((bf16[512,128]{1,0:T(8,128)(2,1)S(1)}, bf16[512,128]{1,0:T(8,128)(2,1)S(1)}, u32[]{:S(2)}, u32[]{:S(2)}) %collective-permute-start.6) | collective-permute-done | bytes 131104 | tf_op jit(solution)/shard_map/ppermute | solution.py:13
  60.7 31.9 %all-gather.2.cloned.1.call-done = bf16[2,16384,1,128]{3,1,2,0:T(8,128)(2,1)} async-done(((bf16[2,512,1,128]{3,1,2,0:T(8,128)(2,1)}), bf16[2,16384,1,128]{3,1,2,0:T(8,128)(2,1)}) %all-gather.2.cloned.1.call-update) | async-done | bytes 8388624 | tf_op jit(solution)/shard_map/all_gather | solution.py:91
  92.7 5.9 %fusion.90 = (bf16[1,16384,1,128]{3,1,2,0:T(8,128)(2,1)}, bf16[1,16384,1,128]{3,1,2,0:T(8,128)(2,1)}) fusion(bf16[2,16384,1,128]{3,1,2,0:T(8,128)(2,1)} %all-gather.2.cloned.1.call-done), kind=kLoop, calls=%fused_computation.187 | loop fusion | bytes 16777216 | tf_op jit(solution)/shard_map/slice | solution.py:103
  98.5 4.1 gather_fusion.10
  102.7 4.1 gather_fusion.7
  106.8 4.2 gather_fusion.12
  111.0 4.1 gather_fusion.9
  118.2 4.7 %gather_fusion = bf16[48,128,128]{2,1,0:T(8,128)(2,1)} fusion(bf16[128,128,128]{2,1,0:T(8,128)(2,1)} %bitcast.228, s32[1024]{0:T(1024)S(1)} %get-tuple-element.36), kind=kCustom, calls=%fused_computation | custom fusion | bytes 3145920 | tf_op jit(solution)/shard_map/gather | solution.py:102
  122.9 4.2 gather_fusion.3
  137.7 6.6 %fusion.24 = f32[128,6144]{0,1:T(8,128)S(1)} fusion(bf16[6144,128]{1,0:T(8,128)(2,1)} %bitcast.239, f32[128]{0:T(128)} %get-tuple-element.19, s32[128]{0:T(128)} %get-tuple-element.15, s32[6144]{0:T(1024)} %bitcast.253, pred[6144]{0:T(1024)(128)(4,1)} %broadcast_bitcast_fusion.3, bf16[512,128]{1,0:T(8,128)(2,1)} %param.13), kind=kOutput, calls=%fused_computation.51 | convolution fusion | flops 205258752 | bytes 4783104 | tf_op jit(solution)/shard_map/rhd,chd->hrc/dot_general | solution.py:19
  148.5 3.7 convert_element_type.182
  152.2 6.6 %fusion.16 = f32[128,6144]{0,1:T(8,128)S(1)} fusion(bf16[6144,128]{1,0:T(8,128)(2,1)} %bitcast.237, f32[128]{0:T(128)} %get-tuple-element.22, s32[128]{0:T(128)} %get-tuple-element.17, s32[6144]{0:T(1024)} %bitcast.252, pred[6144]{0:T(1024)(128)(4,1)} %broadcast_bitcast_fusion.1, bf16[512,128]{1,0:T(8,128)(2,1)} %param.13), kind=kOutput, calls=%fused_computation.41 | convolution fusion | flops 205258752 | bytes 4783104 | tf_op jit(solution)/shard_map/rhd,chd->hrc/dot_general | solution.py:19
  164.2 3.7 convert_element_type.192
  167.9 7.4 %fusion.12 = f32[128,6144]{0,1:T(8,128)S(1)} fusion(bf16[6144,128]{1,0:T(8,128)(2,1)} %bitcast.235, f32[128]{0:T(128)} %get-tuple-element.21, s32[128]{0:T(128)} %get-tuple-element.16, s32[6144]{0:T(1024)} %bitcast.251, pred[6144]{0:T(1024)(128)(4,1)S(1)} %broadcast_bitcast_fusion, bf16[512,128]{1,0:T(8,128)(2,1)} %param.13), kind=kOutput, calls=%fused_computation.36 | convolution fusion | flops 205258752 | bytes 4783104 | tf_op jit(solution)/shard_map/rhd,chd->hrc/dot_general | solution.py:19
  180.7 3.9 convert_element_type.197
  190.4 4.6 convolution_add_fusion.3
  195.0 9.3 %reshape.472 = f32[16384,1,128]{2,0,1:T(8,128)} reshape(f32[128,16384]{1,0:T(8,128)} %convolution_add_fusion.3) | data formatting | bytes 16777216 | tf_op jit(solution)/shard_map/reshape | solution.py:125
  204.3 3.6 fusion.34
  210.5 3.7 convert_element_type.208
  214.2 3.8 fusion.33
  220.6 3.7 convert_element_type.203
  224.4 3.7 fusion.35
  230.7 3.7 convert_element_type.213
  234.4 3.7 fusion.36
  240.6 3.9 convert_element_type.218
  253.6 7.4 %reshape.474 = bf16[32,512,1,128]{3,1,0,2:T(8,128)(2,1)} reshape(bf16[128,16384]{1,0:T(8,128)(2,1)} %fusion) | data formatting | bytes 8388608 | tf_op jit(solution)/shard_map/reshape | solution.py:126
  261.1 6.7 %all-to-all-start = ((bf16[32,512,1,128]{3,1,2,0:T(8,128)(2,1)}), bf16[32,512,1,128]{3,1,2,0:T(8,128)(2,1)}, u32[]{:S(2)}, u32[]{:S(2)}) async-start(bf16[32,512,1,128]{3,1,2,0:T(8,128)(2,1)} %bitcast.229), calls=%async_computation.1 | async-start | bytes 8388608 | tf_op jit(solution)/shard_map/all_to_all | solution.py:127
  274.8 113.8 %all-to-all-done = bf16[32,512,1,128]{3,1,2,0:T(8,128)(2,1)} async-done(((bf16[32,512,1,128]{3,1,2,0:T(8,128)(2,1)}), bf16[32,512,1,128]{3,1,2,0:T(8,128)(2,1)}, u32[]{:S(2)}, u32[]{:S(2)}) %all-to-all-start) | async-done | bytes 4194336 | tf_op jit(solution)/shard_map/all_to_all | solution.py:127
  393.6 59.3 %all_to_all.10 = f32[8,128,512]{1,2,0:T(8,128)S(1)} all-to-all(f32[8,128,512]{1,2,0:T(8,128)S(1)} %bitcast.234), channel_id=1, replica_groups=mesh['seq'=32,'head'=8] {'head'}, dimensions={0} | all-to-all | bytes 4194304 | tf_op jit(solution)/shard_map/all_to_all | solution.py:136
  (163 shorter events, 93.9 us)
Async XLA Ops:
  6.5 267.8 %copy-start = (bf16[1024,128]{1,0:T(8,128)(2,1)S(1)}, bf16[1024,128]{1,0:T(8,128)(2,1)}, u32[]{:S(2)}) copy-start(bf16[1024,128]{1,0:T(8,128)(2,1)} %param.22) | copy-start | bytes 786436
  6.5 17.9 %copy-start.26 = (bf16[512,128]{1,0:T(8,128)(2,1)S(1)}, bf16[512,128]{1,0:T(8,128)(2,1)}, u32[]{:S(2)}) copy-start(bf16[512,128]{1,0:T(8,128)(2,1)} %param.17) | copy-start | bytes 393220
  6.5 14.5 %copy-start.9 = (s32[16384]{0:T(1024)S(1)}, s32[16384]{0:T(1024)}, u32[]{:S(2)}) copy-start(s32[16384]{0:T(1024)} %param.19) | copy-start | bytes 196612
  6.5 14.6 %copy-start.28 = (s32[4]{0:T(128)S(1)}, s32[4]{0:T(128)}, u32[]{:S(2)}) copy-start(s32[4]{0:T(128)} %param.21) | copy-start | bytes 52
  6.5 86.1 %all-gather.2.cloned.1.call-start = ((), (), s32[]{:S(2)}) async-start(), calls=%async_computation.3 | async-start | bytes 8650752 | tf_op jit(solution)/shard_map/all_gather | solution.py:91
  6.6 18.0 %copy-start.36 = (f32[1,512]{1,0:T(1,128)S(1)}, f32[1,512]{1,0:T(1,128)}, u32[]{:S(2)}) copy-start(f32[1,512]{1,0:T(1,128)} %param.18) | copy-start | bytes 6148
  6.6 18.6 %copy-start.27 = (s32[4,48]{1,0:T(4,128)S(1)}, s32[4,48]{1,0:T(4,128)}, u32[]{:S(2)}) copy-start(s32[4,48]{1,0:T(4,128)} %param.20) | copy-start | bytes 2308
  8.4 383.1 %reduce-scatter.2.cloned.1.call-start = ((), (), s32[]{:S(2)}) async-start(), calls=%async_computation.4 | async-start | bytes 8650752 | tf_op jit(solution)/shard_map/reduce_scatter | solution.py:125
  8.5 44.2 %collective-permute-start.5 = (bf16[512,128]{1,0:T(8,128)(2,1)}, bf16[512,128]{1,0:T(8,128)(2,1)S(1)}, u32[]{:S(2)}, u32[]{:S(2)}) collective-permute-start(bf16[512,128]{1,0:T(8,128)(2,1)} %param.17), channel_id=1, source_target_pairs={{0,6},{1,7},{2,0},{3,1},{4,2},{5,3},{6,4},{7,5},{8,14},{9,15},{10,... | collective-permute-start | bytes 393224 | tf_op jit(solution)/shard_map/ppermute | solution.py:13
  11.3 41.3 %collective-permute-start.4 = (bf16[512,128]{1,0:T(8,128)(2,1)}, bf16[512,128]{1,0:T(8,128)(2,1)S(1)}, u32[]{:S(2)}, u32[]{:S(2)}) collective-permute-start(bf16[512,128]{1,0:T(8,128)(2,1)} %param.17), channel_id=1, source_target_pairs={{0,5},{1,6},{2,7},{3,0},{4,1},{5,2},{6,3},{7,4},{8,13},{9,14},{10,... | collective-permute-start | bytes 393224 | tf_op jit(solution)/shard_map/ppermute | solution.py:13
  16.0 36.5 %collective-permute-start.3 = (bf16[512,128]{1,0:T(8,128)(2,1)}, bf16[512,128]{1,0:T(8,128)(2,1)S(1)}, u32[]{:S(2)}, u32[]{:S(2)}) collective-permute-start(bf16[512,128]{1,0:T(8,128)(2,1)} %param.17), channel_id=1, source_target_pairs={{0,4},{1,5},{2,6},{3,7},{4,0},{5,1},{6,2},{7,3},{8,12},{9,13},{10,... | collective-permute-start | bytes 393224 | tf_op jit(solution)/shard_map/ppermute | solution.py:13
  18.8 21.7 %collective-permute-start.1 = (bf16[512,128]{1,0:T(8,128)(2,1)}, bf16[512,128]{1,0:T(8,128)(2,1)S(1)}, u32[]{:S(2)}, u32[]{:S(2)}) collective-permute-start(bf16[512,128]{1,0:T(8,128)(2,1)} %param.17), channel_id=1, source_target_pairs={{0,2},{1,3},{2,4},{3,5},{4,6},{5,7},{6,0},{7,1},{8,10},{9,11},{10,... | collective-permute-start | bytes 393224 | tf_op jit(solution)/shard_map/ppermute | solution.py:13
  18.8 16.2 %collective-permute-start = (bf16[512,128]{1,0:T(8,128)(2,1)}, bf16[512,128]{1,0:T(8,128)(2,1)S(1)}, u32[]{:S(2)}, u32[]{:S(2)}) collective-permute-start(bf16[512,128]{1,0:T(8,128)(2,1)} %param.17), channel_id=1, source_target_pairs={{0,1},{1,2},{2,3},{3,4},{4,5},{5,6},{6,7},{7,0},{8,9},{9,10},{10,1... | collective-permute-start | bytes 393224 | tf_op jit(solution)/shard_map/ppermute | solution.py:13
  20.0 13.3 %copy-start.25 = (bf16[512,128]{1,0:T(8,128)(2,1)S(1)}, bf16[512,128]{1,0:T(8,128)(2,1)}, u32[]{:S(2)}) copy-start(bf16[512,128]{1,0:T(8,128)(2,1)} %param.16) | copy-start | bytes 393220
  34.9 17.6 %collective-permute-start.2 = (bf16[512,128]{1,0:T(8,128)(2,1)S(1)}, bf16[512,128]{1,0:T(8,128)(2,1)S(1)}, u32[]{:S(2)}, u32[]{:S(2)}) collective-permute-start(bf16[512,128]{1,0:T(8,128)(2,1)S(1)} %copy-done.26), channel_id=1, source_target_pairs={{0,3},{1,4},{2,5},{3,6},{4,7},{5,0},{6,1},{7,2},{8,11},{9,12},{10,... | collective-permute-start | bytes 393224 | tf_op jit(solution)/shard_map/ppermute | solution.py:13
  40.5 19.1 %collective-permute-start.6 = (bf16[512,128]{1,0:T(8,128)(2,1)S(1)}, bf16[512,128]{1,0:T(8,128)(2,1)S(1)}, u32[]{:S(2)}, u32[]{:S(2)}) collective-permute-start(bf16[512,128]{1,0:T(8,128)(2,1)S(1)} %copy-done.26), channel_id=1, source_target_pairs={{0,7},{1,0},{2,1},{3,2},{4,3},{5,4},{6,5},{7,6},{8,15},{9,8},{10,9... | collective-permute-start | bytes 393224 | tf_op jit(solution)/shard_map/ppermute | solution.py:13
  118.2 12.0 %copy-start.13 = (bf16[48,128,128]{2,1,0:T(8,128)(2,1)}, bf16[48,128,128]{2,1,0:T(8,128)(2,1)S(1)}, u32[]{:S(2)}) copy-start(bf16[48,128,128]{2,1,0:T(8,128)(2,1)S(1)} %gather_fusion.4) | copy-start | bytes 4718596
  130.2 2.5 copy-start.35
  137.7 6.6 %copy-start.16 = (bf16[48,128,128]{2,1,0:T(8,128)(2,1)S(1)}, bf16[48,128,128]{2,1,0:T(8,128)(2,1)}, u32[]{:S(2)}) copy-start(bf16[48,128,128]{2,1,0:T(8,128)(2,1)} %gather_fusion.3) | copy-start | bytes 4718596
  137.7 6.6 %copy-start.34 = (f32[128]{0:T(128)S(1)}, f32[128]{0:T(128)}, u32[]{:S(2)}) copy-start(f32[128]{0:T(128)} %get-tuple-element.11) | copy-start | bytes 1540
  152.2 6.6 %copy-start.15 = (bf16[48,128,128]{2,1,0:T(8,128)(2,1)S(1)}, bf16[48,128,128]{2,1,0:T(8,128)(2,1)}, u32[]{:S(2)}) copy-start(bf16[48,128,128]{2,1,0:T(8,128)(2,1)} %gather_fusion.9) | copy-start | bytes 4718596
  152.2 6.6 %copy-start.33 = (f32[128]{0:T(128)S(1)}, f32[128]{0:T(128)}, u32[]{:S(2)}) copy-start(f32[128]{0:T(128)} %get-tuple-element.13) | copy-start | bytes 1540
  167.9 7.5 %copy-start.14 = (bf16[48,128,128]{2,1,0:T(8,128)(2,1)S(1)}, bf16[48,128,128]{2,1,0:T(8,128)(2,1)}, u32[]{:S(2)}) copy-start(bf16[48,128,128]{2,1,0:T(8,128)(2,1)} %gather_fusion.12) | copy-start | bytes 4718596
  167.9 7.5 %copy-start.32 = (f32[128]{0:T(128)S(1)}, f32[128]{0:T(128)}, u32[]{:S(2)}) copy-start(f32[128]{0:T(128)} %get-tuple-element.12) | copy-start | bytes 1540
  180.7 3.9 copy-start.31
  184.6 2.9 copy-start.18
  184.6 2.9 copy-start.30
  244.6 2.9 copy-start.19
  261.1 127.6 %all-to-all-start = ((bf16[32,512,1,128]{3,1,2,0:T(8,128)(2,1)}), bf16[32,512,1,128]{3,1,2,0:T(8,128)(2,1)}, u32[]{:S(2)}, u32[]{:S(2)}) async-start(bf16[32,512,1,128]{3,1,2,0:T(8,128)(2,1)} %bitcast.229), calls=%async_computation.1 | async-start | bytes 8388608 | tf_op jit(solution)/shard_map/all_to_all | solution.py:127
  267.8 2.2 copy-start.12
  271.8 1.9 copy-start.10
  274.8 116.7 %copy-start.23 = (bf16[1024,128]{1,0:T(8,128)(2,1)S(1)}, bf16[1024,128]{1,0:T(8,128)(2,1)}, u32[]{:S(2)}) copy-start(bf16[1024,128]{1,0:T(8,128)(2,1)} %param.23) | copy-start | bytes 786436
  (15 other events, 22.4 us)
Sparse Core Ops, SparseCore 0:
  9.2 83.3 all-gather.1
  204.4 167.3 reduce-scatter.1

commit v4 on v2

--- a/solution.py
+++ b/solution.py
@@ -88,30 +88,30 @@
         (key_tiles[:, :, None] == tile_range[None, None, :]) & slots[:, :, None], axis=1
     )
 
-    def visit(key_block, value_block, first_tile):
-        block_tiles = key_block.shape[0] // TILE
-        listed = lax.dynamic_slice(allowed, (0, first_tile), (tiles_here, block_tiles))
-        trace_keys = lax.dynamic_slice_in_dim(trace_id, first_tile * TILE, key_block.shape[0], 0)
-        admit = jnp.repeat(jnp.repeat(listed, TILE, axis=0), TILE, axis=1) & (
-            trace_here[:, None] != trace_keys[None, :]
+    kv_all = lax.all_gather(jnp.stack([key_heads, value_heads]), "seq", axis=1, tiled=True)
+    chunks = 8
+    width_here = tokens_here // chunks
+    kv_split = kv_all.reshape((2, seq_count, chunks, width_here) + kv_all.shape[2:])
+    trace_split = trace_id.reshape(seq_count, chunks, width_here)
+    allowed_split = allowed.reshape(tiles_here, seq_count, tiles_here)
+    query_sum = None
+    sum_parts = []
+    for part in range(chunks):
+        key_block = kv_split[0, :, part].reshape((seq_count * width_here,) + kv_all.shape[2:])
+        value_block = kv_split[1, :, part].reshape((seq_count * width_here,) + kv_all.shape[2:])
+        listed = allowed_split[:, :, (part * width_here) // TILE]
+        admit = jnp.repeat(jnp.repeat(listed, TILE, axis=0), width_here, axis=1) & (
+            trace_here[:, None] != trace_split[:, part].reshape(-1)[None, :]
         )
-        return pair_grads(query_heads, key_block, value_block, grad_heads, lse, delta, admit)
-
-    kv_all = lax.all_gather(jnp.stack([key_heads, value_heads]), "seq", axis=1, tiled=True)
-    total_tokens = kv_all.shape[1]
-    chunk = min(total_tokens, 2048)
-    query_sum = None
-    key_parts, value_parts = [], []
-    for first in range(0, total_tokens, chunk):
-        query_add, key_add, value_add = visit(
-            kv_all[0, first:first + chunk], kv_all[1, first:first + chunk], first // TILE
+        query_add, key_add, value_add = pair_grads(
+            query_heads, key_block, value_block, grad_heads, lse, delta, admit
         )
         query_sum = query_add if query_sum is None else query_sum + query_add
-        key_parts.append(key_add)
-        value_parts.append(value_add)
-    parts = jnp.stack([jnp.concatenate(key_parts), jnp.concatenate(value_parts)])
-    parts = parts.astype(jnp.bfloat16).reshape((2, seq_count, tokens_here) + parts.shape[2:])
-    sums = lax.all_to_all(parts, "seq", 1, 1, tiled=False).astype(jnp.float32).sum(axis=1)
+        parts = jnp.stack([key_add, value_add]).astype(jnp.bfloat16)
+        parts = parts.reshape((2, seq_count, width_here) + kv_all.shape[2:])
+        got = lax.all_to_all(parts, "seq", 1, 1, tiled=False)
+        sum_parts.append(got.astype(jnp.float32).sum(axis=1))
+    sums = jnp.concatenate(sum_parts, axis=1)
     key_sum, value_sum = (sums[0], sums[1])
     d_query = query_sum.astype(jnp.bfloat16).reshape(tokens_here, width)
     d_key = key_sum.astype(jnp.bfloat16).reshape(tokens_here, width)

time: 437 us -> 449 us (1.027)
  waiting for transfers between devices: 219 us -> 137 us
  local copies, waits for them, and re-layouts: 19.9 us -> 65.4 us
  starting transfers between devices: 26.5 us -> 71.3 us
  blocking collectives: 56.4 us -> 62.9 us
    all_to_all x1 -> x8, waiting for transfers between devices: 167 us -> 79.8 us  [per_device(): got = lax.all_to_all(parts, 'seq', 1, 1, tiled=False)]
    all_to_all x1 -> x8, starting transfers between devices: 5.77 us -> 52.2 us  [per_device(): got = lax.all_to_all(parts, 'seq', 1, 1, tiled=False)]
    unnamed x89 -> x102, local copies, waits for them, and re-layouts: 9.18 us -> 28.4 us
    transpose x0 -> x8, local copies, waits for them, and re-layouts: none -> 15.4 us  [pair_grads(): jnp.einsum('hrc,rhd->chd', probs.astype(jnp.bfloat16), grad_heads, prefer...]
    dot_general x7, matrix products: 12 us -> 4.32 us  [pair_grads(): jnp.einsum('hrc,chd->rhd', score_grad, key_heads, preferred_element_type=...]
    ppermute x7, waiting for transfers between devices: 14 us -> 21.6 us  [from_behind(): lax.ppermute(value, axis, [(i, (i + by) % count) for i in range(count)])]
    dot_general x8, matrix products: 16.3 us -> 23.5 us  [pair_grads(): jnp.einsum('rhd,chd->hrc', grad_heads, value_heads, preferred_element_typ...]
    slice x0 -> x3, local copies, waits for them, and re-layouts: none -> 6.92 us  [the longest x1 6.43 us: per_device(): kv_split[1, :, part].reshape((seq_count * width_here,) + kv_all.shape[2:])]
  transfers between devices with their start and end apart: 9 -> 16, of which waited for: 5 -> 12; matrix products, arithmetic and copies ran while one was open for 6% -> 26% of each run, Pallas kernels for 0% -> 0%
where the time goes in v4:
time: 449 us; the launch traced here: 442 us
  waiting for transfers between devices  137 us (31%)
  matrix products  72.9 us (16%)
  starting transfers between devices  71.3 us (16%)
  local copies, waits for them, and re-layouts  65.4 us (15%)
  blocking collectives  62.9 us (14%)
  other arithmetic  17.7 us (4%)
  between operations  14.6 us (3%)
    all_to_all x8, waiting for transfers between devices, per_device(): got = lax.all_to_all(parts, 'seq', 1, 1, tiled=False)  79.8 us
    all_to_all x1, blocking collectives, per_device(): d_input = lax.all_to_all(total, 'head', 0, 0, tiled=False).sum(axis=0)  62.9 us
    all_to_all x8, starting transfers between devices, per_device(): got = lax.all_to_all(parts, 'seq', 1, 1, tiled=False)  52.2 us
    all_gather x1, waiting for transfers between devices, per_device(): lax.all_gather(jnp.stack([key_heads, value_heads]), 'seq', axis=1, tiled=...  35.4 us
    unnamed x102, local copies, waits for them, and re-layouts  28.4 us
    dot_general x8, matrix products, pair_grads(): jnp.einsum('rhd,chd->hrc', grad_heads, value_heads, preferred_element_typ...  23.5 us
    ppermute x7, waiting for transfers between devices, from_behind(): lax.ppermute(value, axis, [(i, (i + by) % count) for i in range(count)])  21.6 us
    ppermute x7, starting transfers between devices, from_behind(): lax.ppermute(value, axis, [(i, (i + by) % count) for i in range(count)])  19 us
  transfers between devices with their start and end apart: 16, of which 12 were waited for; matrix products, arithmetic and copies ran while one was open for 26% of the time, Pallas kernels for 0%

profile of v4, /device:TPU:32, one launch (start us, length us, event | category | flops | bytes accessed | tf_op | source)
XLA Modules:
  0.0 441.5 jit_solution(17007881951600713875)
XLA Ops:
  11.2 6.5 %collective-permute-start.4 = (bf16[512,128]{1,0:T(8,128)(2,1)}, bf16[512,128]{1,0:T(8,128)(2,1)S(1)}, u32[]{:S(2)}, u32[]{:S(2)}) collective-permute-start(bf16[512,128]{1,0:T(8,128)(2,1)} %param.17), channel_id=1, source_target_pairs={{0,5},{1,6},{2,7},{3,0},{4,1},{5,2},{6,3},{7,4},{8,13},{9,14},{10,... | collective-permute-start | bytes 393224 | tf_op jit(solution)/shard_map/ppermute | solution.py:13
  28.4 7.8 %collective-permute-done = bf16[512,128]{1,0:T(8,128)(2,1)S(1)} collective-permute-done((bf16[512,128]{1,0:T(8,128)(2,1)}, bf16[512,128]{1,0:T(8,128)(2,1)S(1)}, u32[]{:S(2)}, u32[]{:S(2)}) %collective-permute-start) | collective-permute-done | bytes 131104 | tf_op jit(solution)/shard_map/ppermute | solution.py:13
  36.2 3.5 collective-permute-start.2
  39.7 3.5 collective-permute-start.6
  43.2 10.7 %collective-permute-done.2 = bf16[512,128]{1,0:T(8,128)(2,1)S(1)} collective-permute-done((bf16[512,128]{1,0:T(8,128)(2,1)S(1)}, bf16[512,128]{1,0:T(8,128)(2,1)S(1)}, u32[]{:S(2)}, u32[]{:S(2)}) %collective-permute-start.2) | collective-permute-done | bytes 131104 | tf_op jit(solution)/shard_map/ppermute | solution.py:13
  54.2 3.1 collective-permute-done.6
  57.8 35.4 %all-gather.2.cloned.1.call-done = bf16[2,16384,1,128]{3,1,2,0:T(8,128)(2,1)} async-done(((bf16[2,512,1,128]{3,1,2,0:T(8,128)(2,1)}), bf16[2,16384,1,128]{3,1,2,0:T(8,128)(2,1)}) %all-gather.2.cloned.1.call-update) | async-done | bytes 8388624 | tf_op jit(solution)/shard_map/all_gather | solution.py:91
  93.2 6.4 %fusion.25 = (bf16[1,32,1,64,1,128]{5,3,2,1,0,4:T(8,128)(2,1)}, bf16[1,32,1,64,1,128]{5,3,2,1,0,4:T(8,128)(2,1)S(1)}, bf16[1,32,1,64,1,128]{5,3,2,1,0,4:T(8,128)...) fusion(bf16[2,32,8,64,1,128]{5,3,2,1,0,4:T(8,128)(2,1)} %bitcas, ...), kind=kLoop, calls=%fused_computation.139 | loop fusion | bytes 16777216 | tf_op jit(solution)/shard_map/slice | solution.py:101
  104.9 3.1 multiply_convert_fusion.1
  109.9 6.3 %all-to-all-start.6 = ((bf16[2,32,64,1,128]{4,2,3,0,1:T(8,128)(2,1)}), bf16[2,32,64,1,128]{4,2,3,0,1:T(8,128)(2,1)}, u32[]{:S(2)}, u32[]{:S(2)}) async-start(bf16[2,32,64,1,128]{4,2,3,0,1:T(8,128)(2,1)} %copy.142), calls=%async_computation.6 | async-start | bytes 2097152 | tf_op jit(solution)/shard_map/all_to_all | solution.py:112
  125.0 3.1 multiply_convert_fusion.2
  131.3 10.6 %all-to-all-done.6 = bf16[2,32,64,1,128]{4,2,3,0,1:T(8,128)(2,1)} async-done(((bf16[2,32,64,1,128]{4,2,3,0,1:T(8,128)(2,1)}), bf16[2,32,64,1,128]{4,2,3,0,1:T(8,128)(2,1)}, u32[]{:S(2)}, u32[]{:S(2)}) %all-to-all-start.6) | async-done | bytes 1048608 | tf_op jit(solution)/shard_map/all_to_all | solution.py:112
  141.9 6.6 %all-to-all-start.5 = ((bf16[2,32,64,1,128]{4,2,3,0,1:T(8,128)(2,1)}), bf16[2,32,64,1,128]{4,2,3,0,1:T(8,128)(2,1)}, u32[]{:S(2)}, u32[]{:S(2)}) async-start(bf16[2,32,64,1,128]{4,2,3,0,1:T(8,128)(2,1)} %copy.140), calls=%async_computation.5 | async-start | bytes 2097152 | tf_op jit(solution)/shard_map/all_to_all | solution.py:112
  156.8 3.1 multiply_convert_fusion.3
  163.2 10.8 %all-to-all-done.5 = bf16[2,32,64,1,128]{4,2,3,0,1:T(8,128)(2,1)} async-done(((bf16[2,32,64,1,128]{4,2,3,0,1:T(8,128)(2,1)}), bf16[2,32,64,1,128]{4,2,3,0,1:T(8,128)(2,1)}, u32[]{:S(2)}, u32[]{:S(2)}) %all-to-all-start.5) | async-done | bytes 1048608 | tf_op jit(solution)/shard_map/all_to_all | solution.py:112
  174.0 6.2 %all-to-all-start.4 = ((bf16[2,32,64,1,128]{4,2,3,0,1:T(8,128)(2,1)}), bf16[2,32,64,1,128]{4,2,3,0,1:T(8,128)(2,1)}, u32[]{:S(2)}, u32[]{:S(2)}) async-start(bf16[2,32,64,1,128]{4,2,3,0,1:T(8,128)(2,1)} %copy.138), calls=%async_computation.4 | async-start | bytes 2097152 | tf_op jit(solution)/shard_map/all_to_all | solution.py:112
  188.9 3.1 multiply_convert_fusion.4
  195.2 10.6 %all-to-all-done.4 = bf16[2,32,64,1,128]{4,2,3,0,1:T(8,128)(2,1)} async-done(((bf16[2,32,64,1,128]{4,2,3,0,1:T(8,128)(2,1)}), bf16[2,32,64,1,128]{4,2,3,0,1:T(8,128)(2,1)}, u32[]{:S(2)}, u32[]{:S(2)}) %all-to-all-start.4) | async-done | bytes 1048608 | tf_op jit(solution)/shard_map/all_to_all | solution.py:112
  205.8 6.2 %all-to-all-start.3 = ((bf16[2,32,64,1,128]{4,2,3,0,1:T(8,128)(2,1)}), bf16[2,32,64,1,128]{4,2,3,0,1:T(8,128)(2,1)}, u32[]{:S(2)}, u32[]{:S(2)}) async-start(bf16[2,32,64,1,128]{4,2,3,0,1:T(8,128)(2,1)} %copy.136), calls=%async_computation.3 | async-start | bytes 2097152 | tf_op jit(solution)/shard_map/all_to_all | solution.py:112
  228.0 3.1 multiply_convert_fusion.5
  234.4 2.9 bitcast_select_fusion.6
  237.7 8.0 %all-to-all-start.2 = ((bf16[2,32,64,1,128]{4,2,3,0,1:T(8,128)(2,1)}), bf16[2,32,64,1,128]{4,2,3,0,1:T(8,128)(2,1)}, u32[]{:S(2)}, u32[]{:S(2)}) async-start(bf16[2,32,64,1,128]{4,2,3,0,1:T(8,128)(2,1)} %copy.134), calls=%async_computation.2 | async-start | bytes 2097152 | tf_op jit(solution)/shard_map/all_to_all | solution.py:112
  245.7 3.8 fusion.1
  251.6 3.1 multiply_convert_fusion.6
  263.8 3.0 multiply_convert_fusion.7
  271.2 6.3 %all-to-all-start.1 = ((bf16[2,32,64,1,128]{4,2,3,0,1:T(8,128)(2,1)}), bf16[2,32,64,1,128]{4,2,3,0,1:T(8,128)(2,1)}, u32[]{:S(2)}, u32[]{:S(2)}) async-start(bf16[2,32,64,1,128]{4,2,3,0,1:T(8,128)(2,1)} %copy.132), calls=%async_computation.1 | async-start | bytes 2097152 | tf_op jit(solution)/shard_map/all_to_all | solution.py:112
  286.8 16.4 %all-to-all-done.1 = bf16[2,32,64,1,128]{4,2,3,0,1:T(8,128)(2,1)} async-done(((bf16[2,32,64,1,128]{4,2,3,0,1:T(8,128)(2,1)}), bf16[2,32,64,1,128]{4,2,3,0,1:T(8,128)(2,1)}, u32[]{:S(2)}, u32[]{:S(2)}) %all-to-all-start.1) | async-done | bytes 1048608 | tf_op jit(solution)/shard_map/all_to_all | solution.py:112
  303.1 6.2 %all-to-all-start = ((bf16[2,32,64,1,128]{4,2,3,0,1:T(8,128)(2,1)}), bf16[2,32,64,1,128]{4,2,3,0,1:T(8,128)(2,1)}, u32[]{:S(2)}, u32[]{:S(2)}) async-start(bf16[2,32,64,1,128]{4,2,3,0,1:T(8,128)(2,1)} %copy.130), calls=%async_computation | async-start | bytes 2097152 | tf_op jit(solution)/shard_map/all_to_all | solution.py:112
  322.5 12.5 %all-to-all-done = bf16[2,32,64,1,128]{4,2,3,0,1:T(8,128)(2,1)} async-done(((bf16[2,32,64,1,128]{4,2,3,0,1:T(8,128)(2,1)}), bf16[2,32,64,1,128]{4,2,3,0,1:T(8,128)(2,1)}, u32[]{:S(2)}, u32[]{:S(2)}) %all-to-all-start) | async-done | bytes 1048608 | tf_op jit(solution)/shard_map/all_to_all | solution.py:112
  335.0 6.3 %all-to-all-start.7 = ((bf16[2,32,64,1,128]{4,2,3,0,1:T(8,128)(2,1)}), bf16[2,32,64,1,128]{4,2,3,0,1:T(8,128)(2,1)S(1)}, u32[]{:S(2)}, u32[]{:S(2)}) async-start(bf16[2,32,64,1,128]{4,2,3,0,1:T(8,128)(2,1)} %copy.144), calls=%async_computation.7 | async-start | bytes 2097152 | tf_op jit(solution)/shard_map/all_to_all | solution.py:112
  349.8 17.1 %all-to-all-done.7 = bf16[2,32,64,1,128]{4,2,3,0,1:T(8,128)(2,1)S(1)} async-done(((bf16[2,32,64,1,128]{4,2,3,0,1:T(8,128)(2,1)}), bf16[2,32,64,1,128]{4,2,3,0,1:T(8,128)(2,1)S(1)}, u32[]{:S(2)}, u32[]{:S(2)}) %all-to-all-start.7) | async-done | bytes 1048608 | tf_op jit(solution)/shard_map/all_to_all | solution.py:112
  370.8 62.9 %all_to_all.45 = f32[8,128,512]{1,2,0:T(8,128)S(1)} all-to-all(f32[8,128,512]{1,2,0:T(8,128)S(1)} %bitcast.313), channel_id=1, replica_groups=mesh['seq'=32,'head'=8] {'head'}, dimensions={0} | all-to-all | bytes 4194304 | tf_op jit(solution)/shard_map/all_to_all | solution.py:124
  (216 shorter events, 128.7 us)
Async XLA Ops:
  6.5 307.9 %copy-start = (bf16[1024,128]{1,0:T(8,128)(2,1)S(1)}, bf16[1024,128]{1,0:T(8,128)(2,1)}, u32[]{:S(2)}) copy-start(bf16[1024,128]{1,0:T(8,128)(2,1)} %param.22) | copy-start | bytes 786436
  6.5 29.7 %copy-start.40 = (bf16[512,128]{1,0:T(8,128)(2,1)S(1)}, bf16[512,128]{1,0:T(8,128)(2,1)}, u32[]{:S(2)}) copy-start(bf16[512,128]{1,0:T(8,128)(2,1)} %param.17) | copy-start | bytes 393220
  6.5 21.7 %copy-start.39 = (bf16[512,128]{1,0:T(8,128)(2,1)S(1)}, bf16[512,128]{1,0:T(8,128)(2,1)}, u32[]{:S(2)}) copy-start(bf16[512,128]{1,0:T(8,128)(2,1)} %param.16) | copy-start | bytes 393220
  6.5 86.6 %all-gather.2.cloned.1.call-start = ((), (), s32[]{:S(2)}) async-start(), calls=%async_computation.9 | async-start | bytes 8650752 | tf_op jit(solution)/shard_map/all_gather | solution.py:91
  8.4 45.8 %collective-permute-start.5 = (bf16[512,128]{1,0:T(8,128)(2,1)}, bf16[512,128]{1,0:T(8,128)(2,1)S(1)}, u32[]{:S(2)}, u32[]{:S(2)}) collective-permute-start(bf16[512,128]{1,0:T(8,128)(2,1)} %param.17), channel_id=1, source_target_pairs={{0,6},{1,7},{2,0},{3,1},{4,2},{5,3},{6,4},{7,5},{8,14},{9,15},{10,... | collective-permute-start | bytes 393224 | tf_op jit(solution)/shard_map/ppermute | solution.py:13
  11.2 42.9 %collective-permute-start.4 = (bf16[512,128]{1,0:T(8,128)(2,1)}, bf16[512,128]{1,0:T(8,128)(2,1)S(1)}, u32[]{:S(2)}, u32[]{:S(2)}) collective-permute-start(bf16[512,128]{1,0:T(8,128)(2,1)} %param.17), channel_id=1, source_target_pairs={{0,5},{1,6},{2,7},{3,0},{4,1},{5,2},{6,3},{7,4},{8,13},{9,14},{10,... | collective-permute-start | bytes 393224 | tf_op jit(solution)/shard_map/ppermute | solution.py:13
  17.7 36.3 %collective-permute-start.3 = (bf16[512,128]{1,0:T(8,128)(2,1)}, bf16[512,128]{1,0:T(8,128)(2,1)S(1)}, u32[]{:S(2)}, u32[]{:S(2)}) collective-permute-start(bf16[512,128]{1,0:T(8,128)(2,1)} %param.17), channel_id=1, source_target_pairs={{0,4},{1,5},{2,6},{3,7},{4,0},{5,1},{6,2},{7,3},{8,12},{9,13},{10,... | collective-permute-start | bytes 393224 | tf_op jit(solution)/shard_map/ppermute | solution.py:13
  20.5 19.3 %collective-permute-start.1 = (bf16[512,128]{1,0:T(8,128)(2,1)}, bf16[512,128]{1,0:T(8,128)(2,1)S(1)}, u32[]{:S(2)}, u32[]{:S(2)}) collective-permute-start(bf16[512,128]{1,0:T(8,128)(2,1)} %param.17), channel_id=1, source_target_pairs={{0,2},{1,3},{2,4},{3,5},{4,6},{5,7},{6,0},{7,1},{8,10},{9,11},{10,... | collective-permute-start | bytes 393224 | tf_op jit(solution)/shard_map/ppermute | solution.py:13
  20.5 15.7 %collective-permute-start = (bf16[512,128]{1,0:T(8,128)(2,1)}, bf16[512,128]{1,0:T(8,128)(2,1)S(1)}, u32[]{:S(2)}, u32[]{:S(2)}) collective-permute-start(bf16[512,128]{1,0:T(8,128)(2,1)} %param.17), channel_id=1, source_target_pairs={{0,1},{1,2},{2,3},{3,4},{4,5},{5,6},{6,7},{7,0},{8,9},{9,10},{10,1... | collective-permute-start | bytes 393224 | tf_op jit(solution)/shard_map/ppermute | solution.py:13
  36.2 17.8 %collective-permute-start.2 = (bf16[512,128]{1,0:T(8,128)(2,1)S(1)}, bf16[512,128]{1,0:T(8,128)(2,1)S(1)}, u32[]{:S(2)}, u32[]{:S(2)}) collective-permute-start(bf16[512,128]{1,0:T(8,128)(2,1)S(1)} %copy-done.40), channel_id=1, source_target_pairs={{0,3},{1,4},{2,5},{3,6},{4,7},{5,0},{6,1},{7,2},{8,11},{9,12},{10,... | collective-permute-start | bytes 393224 | tf_op jit(solution)/shard_map/ppermute | solution.py:13
  39.7 17.5 %collective-permute-start.6 = (bf16[512,128]{1,0:T(8,128)(2,1)S(1)}, bf16[512,128]{1,0:T(8,128)(2,1)S(1)}, u32[]{:S(2)}, u32[]{:S(2)}) collective-permute-start(bf16[512,128]{1,0:T(8,128)(2,1)S(1)} %copy-done.40), channel_id=1, source_target_pairs={{0,7},{1,0},{2,1},{3,2},{4,3},{5,4},{6,5},{7,6},{8,15},{9,8},{10,9... | collective-permute-start | bytes 393224 | tf_op jit(solution)/shard_map/ppermute | solution.py:13
  93.2 6.5 %copy-start.9 = (bf16[512,128]{1,0:T(8,128)(2,1)S(1)}, bf16[512,128]{1,0:T(8,128)(2,1)}, u32[]{:S(2)}) copy-start(bf16[512,128]{1,0:T(8,128)(2,1)} %param.13) | copy-start | bytes 393220
  93.2 6.5 %copy-start.38 = (f32[1,512]{1,0:T(1,128)S(1)}, f32[1,512]{1,0:T(1,128)}, u32[]{:S(2)}) copy-start(f32[1,512]{1,0:T(1,128)} %param.18) | copy-start | bytes 6148
  99.6 4.2 copy-start.23
  104.9 3.8 copy-start.32
  109.9 32.0 %all-to-all-start.6 = ((bf16[2,32,64,1,128]{4,2,3,0,1:T(8,128)(2,1)}), bf16[2,32,64,1,128]{4,2,3,0,1:T(8,128)(2,1)}, u32[]{:S(2)}, u32[]{:S(2)}) async-start(bf16[2,32,64,1,128]{4,2,3,0,1:T(8,128)(2,1)} %copy.142), calls=%async_computation.6 | async-start | bytes 2097152 | tf_op jit(solution)/shard_map/all_to_all | solution.py:112
  125.0 5.2 %copy-start.33 = (bf16[2048,1,128]{2,0,1:T(8,128)(2,1)S(1)}, bf16[2048,1,128]{2,0,1:T(8,128)(2,1)}, u32[]{:S(2)}) copy-start(bf16[2048,1,128]{2,0,1:T(8,128)(2,1)} %copy.139) | copy-start | bytes 1572868
  141.9 32.1 %all-to-all-start.5 = ((bf16[2,32,64,1,128]{4,2,3,0,1:T(8,128)(2,1)}), bf16[2,32,64,1,128]{4,2,3,0,1:T(8,128)(2,1)}, u32[]{:S(2)}, u32[]{:S(2)}) async-start(bf16[2,32,64,1,128]{4,2,3,0,1:T(8,128)(2,1)} %copy.140), calls=%async_computation.5 | async-start | bytes 2097152 | tf_op jit(solution)/shard_map/all_to_all | solution.py:112
  156.8 5.2 %copy-start.34 = (bf16[2048,1,128]{2,0,1:T(8,128)(2,1)S(1)}, bf16[2048,1,128]{2,0,1:T(8,128)(2,1)}, u32[]{:S(2)}) copy-start(bf16[2048,1,128]{2,0,1:T(8,128)(2,1)} %copy.137) | copy-start | bytes 1572868
  174.0 31.9 %all-to-all-start.4 = ((bf16[2,32,64,1,128]{4,2,3,0,1:T(8,128)(2,1)}), bf16[2,32,64,1,128]{4,2,3,0,1:T(8,128)(2,1)}, u32[]{:S(2)}, u32[]{:S(2)}) async-start(bf16[2,32,64,1,128]{4,2,3,0,1:T(8,128)(2,1)} %copy.138), calls=%async_computation.4 | async-start | bytes 2097152 | tf_op jit(solution)/shard_map/all_to_all | solution.py:112
  188.9 5.1 %copy-start.35 = (bf16[2048,1,128]{2,0,1:T(8,128)(2,1)S(1)}, bf16[2048,1,128]{2,0,1:T(8,128)(2,1)}, u32[]{:S(2)}) copy-start(bf16[2048,1,128]{2,0,1:T(8,128)(2,1)} %copy.135) | copy-start | bytes 1572868
  205.8 31.9 %all-to-all-start.3 = ((bf16[2,32,64,1,128]{4,2,3,0,1:T(8,128)(2,1)}), bf16[2,32,64,1,128]{4,2,3,0,1:T(8,128)(2,1)}, u32[]{:S(2)}, u32[]{:S(2)}) async-start(bf16[2,32,64,1,128]{4,2,3,0,1:T(8,128)(2,1)} %copy.136), calls=%async_computation.3 | async-start | bytes 2097152 | tf_op jit(solution)/shard_map/all_to_all | solution.py:112
  228.0 5.1 %copy-start.36 = (bf16[2048,1,128]{2,0,1:T(8,128)(2,1)S(1)}, bf16[2048,1,128]{2,0,1:T(8,128)(2,1)}, u32[]{:S(2)}) copy-start(bf16[2048,1,128]{2,0,1:T(8,128)(2,1)} %copy.133) | copy-start | bytes 1572868
  237.7 33.5 %all-to-all-start.2 = ((bf16[2,32,64,1,128]{4,2,3,0,1:T(8,128)(2,1)}), bf16[2,32,64,1,128]{4,2,3,0,1:T(8,128)(2,1)}, u32[]{:S(2)}, u32[]{:S(2)}) async-start(bf16[2,32,64,1,128]{4,2,3,0,1:T(8,128)(2,1)} %copy.134), calls=%async_computation.2 | async-start | bytes 2097152 | tf_op jit(solution)/shard_map/all_to_all | solution.py:112
  251.6 3.8 copy-start.37
  271.2 31.9 %all-to-all-start.1 = ((bf16[2,32,64,1,128]{4,2,3,0,1:T(8,128)(2,1)}), bf16[2,32,64,1,128]{4,2,3,0,1:T(8,128)(2,1)}, u32[]{:S(2)}, u32[]{:S(2)}) async-start(bf16[2,32,64,1,128]{4,2,3,0,1:T(8,128)(2,1)} %copy.132), calls=%async_computation.1 | async-start | bytes 2097152 | tf_op jit(solution)/shard_map/all_to_all | solution.py:112
  280.1 3.5 copy-start.22
  280.1 3.5 copy-start.31
  303.1 31.9 %all-to-all-start = ((bf16[2,32,64,1,128]{4,2,3,0,1:T(8,128)(2,1)}), bf16[2,32,64,1,128]{4,2,3,0,1:T(8,128)(2,1)}, u32[]{:S(2)}, u32[]{:S(2)}) async-start(bf16[2,32,64,1,128]{4,2,3,0,1:T(8,128)(2,1)} %copy.130), calls=%async_computation | async-start | bytes 2097152 | tf_op jit(solution)/shard_map/all_to_all | solution.py:112
  309.4 4.1 copy-start.11
  309.4 4.1 copy-start.25
  335.0 31.9 %all-to-all-start.7 = ((bf16[2,32,64,1,128]{4,2,3,0,1:T(8,128)(2,1)}), bf16[2,32,64,1,128]{4,2,3,0,1:T(8,128)(2,1)S(1)}, u32[]{:S(2)}, u32[]{:S(2)}) async-start(bf16[2,32,64,1,128]{4,2,3,0,1:T(8,128)(2,1)} %copy.144), calls=%async_computation.7 | async-start | bytes 2097152 | tf_op jit(solution)/shard_map/all_to_all | solution.py:112
  (25 other events, 54.9 us)
Sparse Core Ops, SparseCore 0:
  9.2 83.9 all-gather.1

commit v5 on v2

--- a/solution.py
+++ b/solution.py
@@ -121,7 +121,8 @@
     total = total + lax.dot_general(w_key, d_key, contract, preferred_element_type=jnp.float32)
     total = total + lax.dot_general(w_value, d_value, contract, preferred_element_type=jnp.float32)
     total = total.reshape((head_count, total.shape[0] // head_count) + total.shape[1:])
-    d_input = lax.all_to_all(total, "head", 0, 0, tiled=False).sum(axis=0)
+    total = total.astype(jnp.bfloat16)
+    d_input = lax.all_to_all(total, "head", 0, 0, tiled=False).astype(jnp.float32).sum(axis=0)
     return d_input.T.astype(jnp.bfloat16)
 
 

time: 437 us -> 414 us (0.947)
  blocking collectives: 56.4 us -> 36.7 us
    all_to_all x1, blocking collectives: 56.4 us -> 36.7 us  [per_device(): lax.all_to_all(total, 'head', 0, 0, tiled=False).astype(jnp.float32)]
where the time goes in v5:
time: 414 us; the launch traced here: 410 us
  waiting for transfers between devices  219 us (53%)
  matrix products  76.9 us (19%)
  blocking collectives  36.7 us (9%)
  starting transfers between devices  26.5 us (6%)
  local copies, waits for them, and re-layouts  19.9 us (5%)
  other arithmetic  16.8 us (4%)
  between operations  14.4 us (3%)
    all_to_all x1, waiting for transfers between devices, per_device(): lax.all_to_all(parts, 'seq', 1, 1, tiled=False).astype(jnp.float32)  167 us
    all_gather x1, waiting for transfers between devices, per_device(): lax.all_gather(jnp.stack([key_heads, value_heads]), 'seq', axis=1, tiled=...  38.2 us
    all_to_all x1, blocking collectives, per_device(): lax.all_to_all(total, 'head', 0, 0, tiled=False).astype(jnp.float32)  36.7 us
    ppermute x7, starting transfers between devices, from_behind(): lax.ppermute(value, axis, [(i, (i + by) % count) for i in range(count)])  20.7 us
    dot_general x8, matrix products, pair_grads(): jnp.einsum('rhd,chd->hrc', query_heads, key_heads, preferred_element_type...  20.3 us
    dot_general x8, matrix products, pair_grads(): jnp.einsum('hrc,rhd->chd', probs.astype(jnp.bfloat16), grad_heads, prefer...  16.4 us
    dot_general x8, matrix products, pair_grads(): jnp.einsum('rhd,chd->hrc', grad_heads, value_heads, preferred_element_typ...  16.3 us
    ppermute x7, waiting for transfers between devices, from_behind(): lax.ppermute(value, axis, [(i, (i + by) % count) for i in range(count)])  14 us
  transfers between devices with their start and end apart: 9, of which 5 were waited for; matrix products, arithmetic and copies ran while one was open for 6% of the time, Pallas kernels for 0%

profile of v5, /device:TPU:32, one launch (start us, length us, event | category | flops | bytes accessed | tf_op | source)
XLA Modules:
  0.0 410.2 jit_solution(796429931532682132)
XLA Ops:
  8.4 6.4 %collective-permute-start = (bf16[512,128]{1,0:T(8,128)(2,1)}, bf16[512,128]{1,0:T(8,128)(2,1)S(1)}, u32[]{:S(2)}, u32[]{:S(2)}) collective-permute-start(bf16[512,128]{1,0:T(8,128)(2,1)} %param.17), channel_id=1, source_target_pairs={{0,1},{1,2},{2,3},{3,4},{4,5},{5,6},{6,7},{7,0},{8,9},{9,10},{10,1... | collective-permute-start | bytes 393224 | tf_op jit(solution)/shard_map/ppermute | solution.py:13
  17.4 2.0 collective-permute-start.3
  19.4 7.9 %collective-permute-start.4 = (bf16[512,128]{1,0:T(8,128)(2,1)}, bf16[512,128]{1,0:T(8,128)(2,1)S(1)}, u32[]{:S(2)}, u32[]{:S(2)}) collective-permute-start(bf16[512,128]{1,0:T(8,128)(2,1)} %param.17), channel_id=1, source_target_pairs={{0,5},{1,6},{2,7},{3,0},{4,1},{5,2},{6,3},{7,4},{8,13},{9,14},{10,... | collective-permute-start | bytes 393224 | tf_op jit(solution)/shard_map/ppermute | solution.py:13
  41.7 10.9 %collective-permute-done.6 = bf16[512,128]{1,0:T(8,128)(2,1)S(1)} collective-permute-done((bf16[512,128]{1,0:T(8,128)(2,1)S(1)}, bf16[512,128]{1,0:T(8,128)(2,1)S(1)}, u32[]{:S(2)}, u32[]{:S(2)}) %collective-permute-start.6) | collective-permute-done | bytes 131104 | tf_op jit(solution)/shard_map/ppermute | solution.py:13
  53.1 38.2 %all-gather.2.cloned.1.call-done = bf16[2,16384,1,128]{3,1,2,0:T(8,128)(2,1)} async-done(((bf16[2,512,1,128]{3,1,2,0:T(8,128)(2,1)}), bf16[2,16384,1,128]{3,1,2,0:T(8,128)(2,1)}) %all-gather.2.cloned.1.call-update) | async-done | bytes 8388624 | tf_op jit(solution)/shard_map/all_gather | solution.py:100
  91.4 2.5 bitcast_select_fusion.7
  93.9 2.1 fusion.17
  96.1 2.5 bitcast_select_fusion.6
  98.6 2.1 fusion.19
  100.7 2.5 bitcast_select_fusion.5
  103.2 2.1 fusion.21
  105.3 2.5 bitcast_select_fusion.4
  107.9 2.1 fusion.23
  110.0 2.5 bitcast_select_fusion.3
  112.6 2.1 fusion.25
  114.7 2.5 bitcast_select_fusion.2
  117.3 2.2 fusion.27
  119.4 2.5 bitcast_select_fusion.1
  122.0 2.1 fusion.29
  124.1 2.5 bitcast_select_fusion
  126.7 2.0 copy-done.14
  130.3 6.4 %copy.93 = bf16[16384,1,128]{2,0,1:T(8,128)(2,1)} copy(bf16[16384,1,128]{0,2,1:T(8,128)(2,1)} %fusion.31) | data formatting | bytes 8388608 | tf_op jit(solution)/shard_map/stack | solution.py:112
  136.6 3.2 multiply_convert_fusion.7
  141.9 1.9 multiply_convert_fusion.6
  162.1 2.0 copy-done.31
  164.1 7.6 %pad_maximum_fusion = bf16[2,32,512,1,128]{4,2,3,0,1:T(8,128)(2,1)} fusion(bf16[1,32,512,1,128]{4,2,3,0,1:T(8,128)(2,1)} %bitcast.354, bf16[1,32,512,1,128]{4,2,3,0,1:T(8,128)(2,1)} %bitcast.356), kind=kLoop, calls=%fused_computation.1 | loop fusion | flops 4194304 | bytes 16777216 | tf_op jit(solution)/shard_map/stack | solution.py:112
  171.7 5.8 %all-to-all-start = ((bf16[2,32,512,1,128]{4,2,3,0,1:T(8,128)(2,1)}), bf16[2,32,512,1,128]{4,2,3,0,1:T(8,128)(2,1)}, u32[]{:S(2)}, u32[]{:S(2)}) async-start(bf16[2,32,512,1,128]{4,2,3,0,1:T(8,128)(2,1)} %pad_maximum_fusion), calls=%async_computation | async-start | bytes 16777216 | tf_op jit(solution)/shard_map/all_to_all | solution.py:114
  177.5 2.4 fusion.44
  189.7 3.3 fusion.43
  193.1 166.8 %all-to-all-done = bf16[2,32,512,1,128]{4,2,3,0,1:T(8,128)(2,1)} async-done(((bf16[2,32,512,1,128]{4,2,3,0,1:T(8,128)(2,1)}), bf16[2,32,512,1,128]{4,2,3,0,1:T(8,128)(2,1)}, u32[]{:S(2)}, u32[]{:S(2)}) %all-to-all-start) | async-done | bytes 8388640 | tf_op jit(solution)/shard_map/all_to_all | solution.py:114
  359.8 4.8 %reduce.4 = bf16[2,512,128]{2,1,0:T(8,128)(2,1)S(1)} reduce(bf16[2,32,512,1,128]{4,2,3,0,1:T(8,128)(2,1)} %all-to-all-done, bf16[]{:T(256)} %constant.51.clone.1), dimensions={1,3}, to_apply=%region_2.3.clone | reduce | flops 4063232 | bytes 8650754 | tf_op jit(solution)/shard_map/reduce_sum | solution.py:114
  365.8 36.7 %all_to_all.10 = bf16[8,128,512]{1,2,0:T(8,128)(2,1)S(1)} all-to-all(bf16[8,128,512]{1,2,0:T(8,128)(2,1)S(1)} %bitcast.355), channel_id=1, replica_groups=mesh['seq'=32,'head'=8] {'head'}, dimensions={0} | all-to-all | bytes 2097152 | tf_op jit(solution)/shard_map/all_to_all | solution.py:125
  (156 shorter events, 52.5 us)
Async XLA Ops:
  6.5 183.2 %copy-start = (bf16[1024,128]{1,0:T(8,128)(2,1)S(1)}, bf16[1024,128]{1,0:T(8,128)(2,1)}, u32[]{:S(2)}) copy-start(bf16[1024,128]{1,0:T(8,128)(2,1)} %param.22) | copy-start | bytes 786436
  6.5 30.0 %copy-start.35 = (bf16[512,128]{1,0:T(8,128)(2,1)S(1)}, bf16[512,128]{1,0:T(8,128)(2,1)}, u32[]{:S(2)}) copy-start(bf16[512,128]{1,0:T(8,128)(2,1)} %param.17) | copy-start | bytes 393220
  6.5 84.8 %copy-start.16 = (bf16[512,128]{1,0:T(8,128)(2,1)S(1)}, bf16[512,128]{1,0:T(8,128)(2,1)}, u32[]{:S(2)}) copy-start(bf16[512,128]{1,0:T(8,128)(2,1)} %param.13) | copy-start | bytes 393220
  6.5 84.8 %copy-start.34 = (f32[1,512]{1,0:T(1,128)S(1)}, f32[1,512]{1,0:T(1,128)}, u32[]{:S(2)}) copy-start(f32[1,512]{1,0:T(1,128)} %param.18) | copy-start | bytes 6148
  6.5 84.8 %all-gather.2.cloned.1.call-start = ((), (), s32[]{:S(2)}) async-start(), calls=%async_computation.2 | async-start | bytes 8650752 | tf_op jit(solution)/shard_map/all_gather | solution.py:100
  8.4 28.2 %collective-permute-start = (bf16[512,128]{1,0:T(8,128)(2,1)}, bf16[512,128]{1,0:T(8,128)(2,1)S(1)}, u32[]{:S(2)}, u32[]{:S(2)}) collective-permute-start(bf16[512,128]{1,0:T(8,128)(2,1)} %param.17), channel_id=1, source_target_pairs={{0,1},{1,2},{2,3},{3,4},{4,5},{5,6},{6,7},{7,0},{8,9},{9,10},{10,1... | collective-permute-start | bytes 393224 | tf_op jit(solution)/shard_map/ppermute | solution.py:13
  14.7 23.4 %collective-permute-start.1 = (bf16[512,128]{1,0:T(8,128)(2,1)}, bf16[512,128]{1,0:T(8,128)(2,1)S(1)}, u32[]{:S(2)}, u32[]{:S(2)}) collective-permute-start(bf16[512,128]{1,0:T(8,128)(2,1)} %param.17), channel_id=1, source_target_pairs={{0,2},{1,3},{2,4},{3,5},{4,6},{5,7},{6,0},{7,1},{8,10},{9,11},{10,... | collective-permute-start | bytes 393224 | tf_op jit(solution)/shard_map/ppermute | solution.py:13
  16.2 22.2 %collective-permute-start.2 = (bf16[512,128]{1,0:T(8,128)(2,1)}, bf16[512,128]{1,0:T(8,128)(2,1)S(1)}, u32[]{:S(2)}, u32[]{:S(2)}) collective-permute-start(bf16[512,128]{1,0:T(8,128)(2,1)} %param.17), channel_id=1, source_target_pairs={{0,3},{1,4},{2,5},{3,6},{4,7},{5,0},{6,1},{7,2},{8,11},{9,12},{10,... | collective-permute-start | bytes 393224 | tf_op jit(solution)/shard_map/ppermute | solution.py:13
  17.4 21.1 %collective-permute-start.3 = (bf16[512,128]{1,0:T(8,128)(2,1)}, bf16[512,128]{1,0:T(8,128)(2,1)S(1)}, u32[]{:S(2)}, u32[]{:S(2)}) collective-permute-start(bf16[512,128]{1,0:T(8,128)(2,1)} %param.17), channel_id=1, source_target_pairs={{0,4},{1,5},{2,6},{3,7},{4,0},{5,1},{6,2},{7,3},{8,12},{9,13},{10,... | collective-permute-start | bytes 393224 | tf_op jit(solution)/shard_map/ppermute | solution.py:13
  19.4 20.5 %collective-permute-start.4 = (bf16[512,128]{1,0:T(8,128)(2,1)}, bf16[512,128]{1,0:T(8,128)(2,1)S(1)}, u32[]{:S(2)}, u32[]{:S(2)}) collective-permute-start(bf16[512,128]{1,0:T(8,128)(2,1)} %param.17), channel_id=1, source_target_pairs={{0,5},{1,6},{2,7},{3,0},{4,1},{5,2},{6,3},{7,4},{8,13},{9,14},{10,... | collective-permute-start | bytes 393224 | tf_op jit(solution)/shard_map/ppermute | solution.py:13
  36.6 5.0 %collective-permute-start.5 = (bf16[512,128]{1,0:T(8,128)(2,1)S(1)}, bf16[512,128]{1,0:T(8,128)(2,1)S(1)}, u32[]{:S(2)}, u32[]{:S(2)}) collective-permute-start(bf16[512,128]{1,0:T(8,128)(2,1)S(1)} %copy-done.35), channel_id=1, source_target_pairs={{0,6},{1,7},{2,0},{3,1},{4,2},{5,3},{6,4},{7,5},{8,14},{9,15},{10,... | collective-permute-start | bytes 393224 | tf_op jit(solution)/shard_map/ppermute | solution.py:13
  38.1 14.5 %collective-permute-start.6 = (bf16[512,128]{1,0:T(8,128)(2,1)S(1)}, bf16[512,128]{1,0:T(8,128)(2,1)S(1)}, u32[]{:S(2)}, u32[]{:S(2)}) collective-permute-start(bf16[512,128]{1,0:T(8,128)(2,1)S(1)} %copy-done.35), channel_id=1, source_target_pairs={{0,7},{1,0},{2,1},{3,2},{4,3},{5,4},{6,5},{7,6},{8,15},{9,8},{10,9... | collective-permute-start | bytes 393224 | tf_op jit(solution)/shard_map/ppermute | solution.py:13
  93.9 4.7 %copy-start.1 = (f32[512,2048]{0,1:T(8,128)}, f32[512,2048]{0,1:T(8,128)S(1)}, u32[]{:S(2)}) copy-start(f32[512,2048]{0,1:T(8,128)S(1)} %bitcast_select_fusion.7) | copy-start | bytes 12582916
  98.6 4.6 %copy-start.2 = (f32[512,2048]{0,1:T(8,128)}, f32[512,2048]{0,1:T(8,128)S(1)}, u32[]{:S(2)}) copy-start(f32[512,2048]{0,1:T(8,128)S(1)} %bitcast_select_fusion.6) | copy-start | bytes 12582916
  103.2 4.6 %copy-start.4 = (f32[512,2048]{0,1:T(8,128)}, f32[512,2048]{0,1:T(8,128)S(1)}, u32[]{:S(2)}) copy-start(f32[512,2048]{0,1:T(8,128)S(1)} %bitcast_select_fusion.5) | copy-start | bytes 12582916
  107.9 4.7 %copy-start.6 = (f32[512,2048]{0,1:T(8,128)}, f32[512,2048]{0,1:T(8,128)S(1)}, u32[]{:S(2)}) copy-start(f32[512,2048]{0,1:T(8,128)S(1)} %bitcast_select_fusion.4) | copy-start | bytes 12582916
  112.6 4.6 %copy-start.8 = (f32[512,2048]{0,1:T(8,128)}, f32[512,2048]{0,1:T(8,128)S(1)}, u32[]{:S(2)}) copy-start(f32[512,2048]{0,1:T(8,128)S(1)} %bitcast_select_fusion.3) | copy-start | bytes 12582916
  117.2 4.7 %copy-start.10 = (f32[512,2048]{0,1:T(8,128)}, f32[512,2048]{0,1:T(8,128)S(1)}, u32[]{:S(2)}) copy-start(f32[512,2048]{0,1:T(8,128)S(1)} %bitcast_select_fusion.2) | copy-start | bytes 12582916
  122.0 4.7 %copy-start.12 = (f32[512,2048]{0,1:T(8,128)}, f32[512,2048]{0,1:T(8,128)S(1)}, u32[]{:S(2)}) copy-start(f32[512,2048]{0,1:T(8,128)S(1)} %bitcast_select_fusion.1) | copy-start | bytes 12582916
  136.6 5.3 %copy-start.3 = (f32[512,2048]{0,1:T(8,128)S(1)}, f32[512,2048]{0,1:T(8,128)}, u32[]{:S(2)}) copy-start(f32[512,2048]{0,1:T(8,128)} %copy-done.2) | copy-start | bytes 12582916
  147.6 2.9 copy-start.9
  150.5 2.9 copy-start.11
  171.7 188.1 %all-to-all-start = ((bf16[2,32,512,1,128]{4,2,3,0,1:T(8,128)(2,1)}), bf16[2,32,512,1,128]{4,2,3,0,1:T(8,128)(2,1)}, u32[]{:S(2)}, u32[]{:S(2)}) async-start(bf16[2,32,512,1,128]{4,2,3,0,1:T(8,128)(2,1)} %pad_maximum_fusion), calls=%async_computation | async-start | bytes 16777216 | tf_op jit(solution)/shard_map/all_to_all | solution.py:114
  177.5 4.1 copy-start.18
  177.5 5.8 %copy-start.20 = (bf16[512,2048]{0,1:T(8,128)(2,1)S(1)}, bf16[512,2048]{0,1:T(8,128)(2,1)}, u32[]{:S(2)}) copy-start(bf16[512,2048]{0,1:T(8,128)(2,1)} %copy-done.19) | copy-start | bytes 6291460
  179.9 5.1 %copy-start.22 = (bf16[512,2048]{0,1:T(8,128)(2,1)S(1)}, bf16[512,2048]{0,1:T(8,128)(2,1)}, u32[]{:S(2)}) copy-start(bf16[512,2048]{0,1:T(8,128)(2,1)} %copy-done.21) | copy-start | bytes 6291460
  181.6 5.1 %copy-start.24 = (bf16[512,2048]{0,1:T(8,128)(2,1)S(1)}, bf16[512,2048]{0,1:T(8,128)(2,1)}, u32[]{:S(2)}) copy-start(bf16[512,2048]{0,1:T(8,128)(2,1)} %copy-done.23) | copy-start | bytes 6291460
  183.3 4.9 %copy-start.26 = (bf16[512,2048]{0,1:T(8,128)(2,1)S(1)}, bf16[512,2048]{0,1:T(8,128)(2,1)}, u32[]{:S(2)}) copy-start(bf16[512,2048]{0,1:T(8,128)(2,1)} %copy-done.25) | copy-start | bytes 6291460
  185.0 4.8 %copy-start.28 = (bf16[512,2048]{0,1:T(8,128)(2,1)S(1)}, bf16[512,2048]{0,1:T(8,128)(2,1)}, u32[]{:S(2)}) copy-start(bf16[512,2048]{0,1:T(8,128)(2,1)} %copy-done.27) | copy-start | bytes 6291460
  193.1 171.6 %copy-start.32 = (bf16[1024,128]{1,0:T(8,128)(2,1)S(1)}, bf16[1024,128]{1,0:T(8,128)(2,1)}, u32[]{:S(2)}) copy-start(bf16[1024,128]{1,0:T(8,128)(2,1)} %param.23) | copy-start | bytes 786436
  193.1 172.0 %copy-start.30 = (f32[512,1024]{1,0:T(8,128)S(1)}, f32[512,1024]{1,0:T(8,128)}, u32[]{:S(2)}) copy-start(f32[512,1024]{1,0:T(8,128)} %fusion.43) | copy-start | bytes 6291460
  193.1 172.0 %copy-start.33 = (bf16[1024,128]{1,0:T(8,128)(2,1)S(1)}, bf16[1024,128]{1,0:T(8,128)(2,1)}, u32[]{:S(2)}) copy-start(bf16[1024,128]{1,0:T(8,128)(2,1)} %param.24) | copy-start | bytes 786436
  (13 other events, 32.1 us)
Sparse Core Ops, SparseCore 0:
  9.2 82.0 all-gather.1
